TPU v7x, 512 devices: a whole 4x8x8 slice. The times are simulated.
512 devices in a mesh: lat: 16 (over y_hi, x, core), lon: 32 (over z, y_lo).
Axes of the slice: x: 4, y: 8 (y_hi: 2, y_lo: 4; y = y_hi * 4 + y_lo), z: 8, core: 2. Of those that a mesh axis runs over, the one named last changes fastest.
Arguments:
- queries: bfloat16 [131072, 1024], P(('lat', 'lon')), may hold values from -6 to 6
- gain: bfloat16 [1024], replicated, may hold values from 0.099609375 to 1.8984375
- w_query: bfloat16 [1024, 1024], P('lon'), may hold values from -0.1875 to 0.1875
- w_out: bfloat16 [1024, 1024], P(None, 'lon'), may hold values from -0.75 to 0.75
- kv_cache: bfloat16 [2, 32, 256, 1024], P(None, 'lat'), may hold values from -60 to 60
- nbr_lists: int32 [512, 4], P(('lat', 'lon')), may hold values from 0 to 31, as said below
- counts: int32 [512], P(('lat', 'lon')), may hold values from 1 to 4, as said below
Outputs:
- decoded: bfloat16 [131072, 1024], P(('lat', 'lon'))
Inputs may be any that keep to these rules, and one draw needn't show every extreme that they name: `nbr_lists`: query block b lies in band b // 32; band k holds latent blocks k * 2 to (k+1) * 2 - 1. Entries of b's list lie in its band or the bands beside it; its first counts[b] entries differ, the others repeat entry 0. `counts`: query blocks of the first and last band have 4 valid slots.
All inputs are finite; a program needn't handle non-finite values.
Results may differ from a plain program's by a relative error of at most 0.007.
The roundings to bfloat16 on the way count: a program that leaves them out, or rounds other values in their place, can miss the bound.
Values may be sent and summed in bfloat16 or wider, within the bound.
No kernel may reach another device: no remote copies, remote signals or barrier semaphores. Data moves between devices by JAX's collectives and lax.ppermute only.
A program may use at most 64 MiB of HBM per device.

v0:
```python
import jax
import jax.numpy as jnp
from jax import lax
from jax.experimental import pallas as pl
from jax.experimental.pallas import tpu as pltpu
from jax.sharding import PartitionSpec as P


HD = 64


def attention_kernel(slots_ref, count_ref, q_ref, *refs):
    key_refs, value_refs, out_ref = refs[: (len(refs) - 1) // 2], refs[(len(refs) - 1) // 2 : -1], refs[-1]
    count = count_ref[0]
    width = q_ref.shape[1]
    lane = lax.broadcasted_iota(jnp.int32, (1, width), 1)
    q_all = q_ref[...]
    result = None
    for head in range(width // HD):
        in_head = (lane >= head * HD) & (lane < (head + 1) * HD)
        q_head = jnp.where(in_head, q_all, jnp.zeros_like(q_all))
        scores = []
        for slot, key_ref in enumerate(key_refs):
            s = lax.dot_general(q_head, key_ref[...], (((1,), (1,)), ((), ())), preferred_element_type=jnp.float32)
            scores.append(jnp.where(slot < count, s, -jnp.inf))
        peak = scores[0].max(axis=1, keepdims=True)
        for s in scores[1:]:
            peak = jnp.maximum(peak, s.max(axis=1, keepdims=True))
        total = None
        mixed = None
        for s, value_ref in zip(scores, value_refs):
            expo = jnp.exp(s - peak)
            part = expo.sum(axis=1, keepdims=True)
            total = part if total is None else total + part
            term = jnp.dot(expo.astype(jnp.bfloat16), value_ref[...], preferred_element_type=jnp.float32)
            mixed = term if mixed is None else mixed + term
        head_out = mixed / total
        result = head_out if result is None else jnp.where(in_head, head_out, result)
    out_ref[...] = result.astype(out_ref.dtype)


def attend(q, window, slots, count, lanes=128):
    rows, width = q.shape
    nbr = slots.shape[0]
    q_spec = pl.BlockSpec((rows, lanes), lambda h, s, c: (0, h))

    def kv_spec(part, slot):
        return pl.BlockSpec((None, None, rows, lanes), lambda h, s, c: (part, s[slot], 0, h))

    in_specs = [q_spec] + [kv_spec(0, j) for j in range(nbr)] + [kv_spec(1, j) for j in range(nbr)]
    return pl.pallas_call(
        attention_kernel,
        grid_spec=pltpu.PrefetchScalarGridSpec(
            num_scalar_prefetch=2, grid=(width // lanes,), in_specs=in_specs, out_specs=q_spec),
        out_shape=jax.ShapeDtypeStruct((rows, width), jnp.bfloat16),
    )(slots, count, q, *([window] * (2 * nbr)))


Y_LO = 4


def neighbour_bands(kv):
    lat_count, lon_count = lax.axis_size("lat"), lax.axis_size("lon")
    lat, lon = lax.axis_index("lat"), lax.axis_index("lon")
    both = ("lat", "lon")
    split = lat_count // 2
    up = [(k * lon_count + l, (k + 1) * lon_count + l) for k in range(lat_count - 1) if k != split - 1 for l in range(lon_count)]
    below = lax.ppermute(kv, both, up)
    above = lax.ppermute(kv, both, [(j, i) for i, j in up])
    rows = kv.shape[2] // Y_LO
    z = lon // Y_LO
    z_count = lon_count // Y_LO
    piece = lax.dynamic_slice_in_dim(kv, (z % Y_LO) * rows, rows, axis=2)
    cross = []
    for l in range(lon_count):
        mirror = l - l % Y_LO + (Y_LO - 1 - l % Y_LO)
        cross.append(((split - 1) * lon_count + l, split * lon_count + mirror))
        cross.append((split * lon_count + l, (split - 1) * lon_count + mirror))
    own = lax.ppermute(piece, both, cross)

    def along_z(value, shift):
        pairs = []
        for band in (split - 1, split):
            for l in range(lon_count):
                target = ((l // Y_LO + shift) % z_count) * Y_LO + l % Y_LO
                pairs.append((band * lon_count + l, band * lon_count + target))
        return lax.ppermute(value, both, pairs)

    half = rows // 2
    opposite = jnp.concatenate(
        [along_z(own[:, :, :half], 2), along_z(own[:, :, half:], -2)], axis=2
    )
    quarters = jnp.stack([own, along_z(own, -1), opposite, along_z(own, 1)])
    order = (jnp.arange(Y_LO) - z) % Y_LO
    joined = jnp.take(quarters, order, axis=0)
    joined = jnp.moveaxis(joined, 0, 2).reshape(kv.shape)
    below = jnp.where(lat == split, joined, below)
    above = jnp.where(lat == split - 1, joined, above)
    return below, above


def gathered_rows(local, after=None):
    lon_count = lax.axis_size("lon")
    core = lax.axis_index("lat") % 2
    half = local.shape[1] // 2
    mine = lax.dynamic_slice_in_dim(local, core * half, half, axis=1)
    if after is not None:
        mine, _ = lax.optimization_barrier((mine, after))
    fetched = lax.all_to_all(jnp.tile(mine, (lon_count, 1)), "lon", 0, 0, tiled=True)
    lat_count = lax.axis_size("lat")
    swap = [(i, i ^ 1) for i in range(lat_count)]
    other = lax.ppermute(fetched, "lat", swap)
    low = jnp.where(core == 0, fetched, other)
    high = jnp.where(core == 0, other, fetched)
    return jnp.concatenate([low, high], axis=1)


def layer(queries, gain, w_query, w_out, kv_cache, nbr_lists, counts):
    rows = queries.astype(jnp.float32)
    rowwise_scale = lax.rsqrt(jnp.mean(rows * rows, axis=1, keepdims=True) + 1e-05)
    normed = (rows * rowwise_scale * gain.astype(jnp.float32)[None, :]).astype(jnp.bfloat16)
    w_query_rows = gathered_rows(w_query)
    projected = jnp.dot(
        normed,
        w_query_rows,
        preferred_element_type=jnp.float32,
    )
    query = (projected * HD ** (-0.5)).astype(jnp.bfloat16)
    blocks_here = kv_cache.shape[1]
    below, above = neighbour_bands(kv_cache)
    window = jnp.concatenate([below, kv_cache, above], axis=1)
    local_lists = nbr_lists - (lax.axis_index("lat") - 1) * blocks_here
    slots = jnp.clip(local_lists[0], 0, window.shape[1] - 1)
    attended = attend(query, window, slots, counts)
    w_out_rows = gathered_rows(w_out.T, after=query)
    decoded = lax.dot_general(
        attended,
        w_out_rows,
        (((1,), (1,)), ((), ())),
        preferred_element_type=jnp.float32,
    )
    return decoded.astype(jnp.bfloat16)


def solution(mesh):
    placed = (
        P(("lat", "lon"), None),
        P(),
        P("lon", None),
        P(None, "lon"),
        P(None, "lat", None, None),
        P(("lat", "lon"), None),
        P(("lat", "lon")),
    )
    return jax.shard_map(layer, mesh=mesh, in_specs=placed, out_specs=P(("lat", "lon"), None), check_vma=False)
```

profile of v0, /device:TPU:41, one launch (start us, length us, event | category | flops | bytes accessed | tf_op | source)
XLA Modules:
  0.0 138.6 jit_solution(14592581826517041391)
XLA Ops:
  0.0 0.0 copy-start
  0.0 0.0 copy-start.4
  0.0 0.0 copy-start.3
  0.0 0.0 copy-start.2
  0.0 0.8 copy-done
  0.8 0.1 tile.4
  1.0 38.5 %all_to_all.18 = bf16[32,32,512]{2,1,0:T(8,128)(2,1)S(1)} all-to-all(bf16[32,32,512]{2,1,0:T(8,128)(2,1)S(1)} %tile.4), channel_id=1, replica_groups=mesh['lat'=16,'lon'=32] {'lon'}, dimensions={0} | all-to-all | bytes 2097152 | tf_op jit(solution)/shard_map/all_to_all | solution.py:109
  39.4 3.5 %collective-permute-start = (bf16[1024,512]{1,0:T(8,128)(2,1)S(1)}, bf16[1024,512]{1,0:T(8,128)(2,1)S(1)}, u32[]{:S(2)}, u32[]{:S(2)}) collective-permute-start(bf16[1024,512]{1,0:T(8,128)(2,1)S(1)} %bitcast.24), channel_id=1, source_target_pairs={{0,32},{32,0},{64,96},{96,64},{128,160},{160,128},{192,224},{224,1... | collective-permute-start | bytes 3145736 | tf_op jit(solution)/shard_map/ppermute | solution.py:112
  43.0 0.0 copy-done.4
  43.0 0.0 copy-done.3
  43.0 0.0 copy-done.2
  43.0 0.2 fusion.17
  43.2 2.0 %collective-permute-done = bf16[1024,512]{1,0:T(8,128)(2,1)S(1)} collective-permute-done((bf16[1024,512]{1,0:T(8,128)(2,1)S(1)}, bf16[1024,512]{1,0:T(8,128)(2,1)S(1)}, u32[]{:S(2)}, u32[]{:S(2)}) %collective-permute-start) | collective-permute-done | bytes 1048608 | tf_op jit(solution)/shard_map/ppermute | solution.py:112
  45.2 0.2 broadcast_select_fusion.3
  45.5 1.6 %fusion.11.q_ref = bf16[256,1024]{1,0:T(8,128)(2,1)} fusion(bf16[1024,512]{1,0:T(8,128)(2,1)S(1)} %get-tuple-element.12, bf16[1024,512]{1,0:T(8,128)(2,1)S(1)} %get-tuple-element.11, bf16[256,1024]{1,0:T(8,128)(2,1)S(1)} %copy-done.2, f32[1024]{0:T(1024)S(1)} %convert_element_type.16, f32[256]{0:T(256)S(1)} %add_rsqrt_fusion), kind=kOutput, calls=%fused_computation.17 | convolution fusion | flops 542638080 | bytes 3150848 | tf_op jit(solution)/shard_map/dot_general | solution.py:123
  47.0 1.1 tile.5
  48.1 5.9 %all-to-all-start.1 = ((bf16[32,32,512]{2,1,0:T(8,128)(2,1)}), bf16[32,32,512]{2,1,0:T(8,128)(2,1)S(1)}, u32[]{:S(2)}, u32[]{:S(2)}) async-start(bf16[32,32,512]{2,1,0:T(8,128)(2,1)} %tile.5), calls=%async_computation.1 | async-start | bytes 2097152 | tf_op jit(solution)/shard_map/all_to_all | solution.py:109
  54.0 4.0 %collective-permute-start.6 = (bf16[2,2,256,1024]{3,2,1,0:T(8,128)(2,1)}, bf16[2,2,256,1024]{3,2,1,0:T(8,128)(2,1)}, u32[]{:S(2)}, u32[]{:S(2)}) collective-permute-start(bf16[2,2,256,1024]{3,2,1,0:T(8,128)(2,1)} %param.11), channel_id=1, source_target_pairs={{0,32},{1,33},{2,34},{3,35},{4,36},{5,37},{6,38},{7,39},{8,40},{9,... | collective-permute-start | bytes 6291464 | tf_op jit(solution)/shard_map/ppermute | solution.py:68
  58.0 1.9 %collective-permute-start.7 = (bf16[2,2,256,1024]{3,2,1,0:T(8,128)(2,1)}, bf16[2,2,256,1024]{3,2,1,0:T(8,128)(2,1)}, u32[]{:S(2)}, u32[]{:S(2)}) collective-permute-start(bf16[2,2,256,1024]{3,2,1,0:T(8,128)(2,1)} %param.11), channel_id=1, source_target_pairs={{32,0},{33,1},{34,2},{35,3},{36,4},{37,5},{38,6},{39,7},{40,8},{41... | collective-permute-start | bytes 6291464 | tf_op jit(solution)/shard_map/ppermute | solution.py:69
  60.0 1.1 constant_dynamic-slice_fusion
  61.0 0.7 collective-permute-start.1
  61.7 0.0 collective-permute-done.1
  61.8 0.7 collective-permute-start.3
  62.5 0.7 collective-permute-start.2
  63.2 0.7 collective-permute-start.5
  63.9 0.0 collective-permute-done.3
  63.9 1.4 collective-permute-start.4
  66.0 0.0 copy-done.5
  66.0 0.5 clamp_bitcast_fusion.slots_ref
  66.5 0.0 collective-permute-done.4
  66.5 1.0 maximum_bitcast_fusion
  67.5 0.0 collective-permute-done.2
  67.5 0.0 collective-permute-done.5
  67.5 1.6 %pad_maximum_fusion.1 = bf16[4,2,2,64,1024]{4,3,2,1,0:T(8,128)(2,1)} fusion(bf16[1,2,2,64,1024]{4,3,2,1,0:T(8,128)(2,1)S(1)} %bitcast.27, bf16[1,2,2,64,1024]{4,3,2,1,0:T(8,128)(2,1)S(1)} %maximum_bitcast_fusion, bf16[1,2,2,64,1024]{4,3,2,1,0:T(8,128)(2,1)S(1)} %bitcast.26, bf16[1,2,2,64,1024]{4,3,2,1,0:T(8,128)(2,1)S(1)} %bitcast.25), kind=kLoop, calls=%fused_computation.6 | loop fusion | flops 3145728 | bytes 4194304 | tf_op jit(solution)/shard_map/stack | solution.py:93
  69.1 2.3 %gather_fusion = bf16[4,2,2,64,1024]{4,3,2,1,0:T(8,128)(2,1)S(1)} fusion(bf16[4,2,2,64,1024]{4,3,2,1,0:T(8,128)(2,1)} %pad_maximum_fusion.1, s32[1024]{0:T(1024)S(1)} %pad_clamp_fusion), kind=kCustom, calls=%fused_computation | custom fusion | bytes 4194320 | tf_op jit(solution)/shard_map/jit(_take)/gather | solution.py:95
  71.4 10.0 %all-to-all-done.1 = bf16[32,32,512]{2,1,0:T(8,128)(2,1)S(1)} async-done(((bf16[32,32,512]{2,1,0:T(8,128)(2,1)}), bf16[32,32,512]{2,1,0:T(8,128)(2,1)S(1)}, u32[]{:S(2)}, u32[]{:S(2)}) %all-to-all-start.1) | async-done | bytes 1048608 | tf_op jit(solution)/shard_map/all_to_all | solution.py:109
  81.4 34.6 %collective-permute-start.8 = (bf16[1024,512]{1,0:T(8,128)(2,1)S(1)}, bf16[1024,512]{1,0:T(8,128)(2,1)}, u32[]{:S(2)}, u32[]{:S(2)}) collective-permute-start(bf16[1024,512]{1,0:T(8,128)(2,1)S(1)} %bitcast.23), channel_id=1, source_target_pairs={{0,32},{32,0},{64,96},{96,64},{128,160},{160,128},{192,224},{224,1... | collective-permute-start | bytes 3145736 | tf_op jit(solution)/shard_map/ppermute | solution.py:112
  116.0 0.3 select_bitcast_fusion
  116.2 0.3 copy.8
  116.5 0.0 collective-permute-done.6
  116.5 0.0 collective-permute-done.7
  116.5 2.6 %bitcast_select_fusion.1 = (bf16[2,2,256,1024]{3,2,1,0:T(8,128)(2,1)S(1)}, bf16[2,2,256,1024]{3,2,1,0:T(8,128)(2,1)S(1)}) fusion(bf16[2,2,256,1024]{3,2,1,0:T(8,128)(2,1)} %collective-permute-done.6, bf16[2,2,4,64,1024]{4,3,2,1,0:T(8,128)(2,1)S(1)} %copy.8, pred[]{:T(512)S(6)} %eq.19, bf16[2,2,256,1024]{3,2,1,0:T(8,128)(2,1)} %collective-permute-done.7, ...), kind=kLoop, calls=%fused_computation.12 | loop fusion | flops 2097152 | bytes 10485762 | tf_op jit(solution)/shard_map/jit(_where)/select_n | solution.py:97
  119.1 4.5 %pad_maximum_fusion.refs_0_.refs_1_.refs_2_.refs_3_.refs_4_.refs_5_.refs_6_.refs_7_ = bf16[2,6,256,1024]{3,2,1,0:T(8,128)(2,1)} fusion(bf16[2,2,256,1024]{3,2,1,0:T(8,128)(2,1)S(1)} %get-tuple-element.10, bf16[2,2,256,1024]{3,2,1,0:T(8,128)(2,1)} %param.11, bf16[2,2,256,1024]{3,2,1,0:T(8,128)(2,1)S(1)} %get-tuple-element.9), kind=kLoop, calls=%fused_computation.1 | loop fusion | flops 6291456 | bytes 12582912 | tf_op jit(solution)/shard_map/concatenate | solution.py:131
  123.7 12.0 %shard_map.73 = bf16[256,1024]{1,0:T(8,128)(2,1)} custom-call(s32[4]{0:T(128)} %clamp_bitcast_fusion.slots_ref, s32[1]{0:T(128)S(6)} %copy.9.count_ref, bf16[256,1024]{1,0:T(8,128)(2,1)} %fusion.11.q_ref, bf16[2,6,256,1024]{3,2,1,0:T(8,128)(2,1)} %pad_maximum_fusion.refs_0_.refs_1_.refs_2_.refs_3_.refs_4_.refs_5_.refs_6_.refs_7_, ...), custom_call_target="tpu_custom_call" | custom-call | tf_op jit(solution)/shard_map/pallas_call | solution.py:51
  135.7 0.0 collective-permute-done.8
  135.7 1.4 %broadcast_select_fusion.1 = (bf16[1024,512]{1,0:T(8,128)(2,1)S(1)}, bf16[1024,512]{1,0:T(8,128)(2,1)S(1)}) fusion(bf16[1024,512]{1,0:T(8,128)(2,1)} %collective-permute-done.8, pred[]{:T(512)S(6)} %eq.18, bf16[32,32,512]{2,1,0:T(8,128)(2,1)S(1)} %all-to-all-done.1), kind=kLoop, calls=%fused_computation.23 | loop fusion | flops 1048576 | bytes 4194305 | tf_op jit(solution)/shard_map/jit(_where)/select_n | solution.py:113
  137.1 0.0 copy-done.1
  137.1 1.5 %fusion.14 = bf16[256,1024]{1,0:T(8,128)(2,1)} fusion(bf16[256,1024]{1,0:T(8,128)(2,1)S(1)} %copy-done.1, bf16[1024,512]{1,0:T(8,128)(2,1)S(1)} %get-tuple-element.8, bf16[1024,512]{1,0:T(8,128)(2,1)S(1)} %get-tuple-element.7), kind=kOutput, calls=%fused_computation.18 | convolution fusion | flops 541327360 | bytes 3145728 | tf_op jit(solution)/shard_map/dot_general | solution.py:136
  (10 shorter events, 0.1 us)
Async XLA Ops:
  0.0 0.8 copy-start
  0.0 43.0 %copy-start.4 = (bf16[1024]{0:T(1024)(128)(2,1)S(1)}, bf16[1024]{0:T(1024)(128)(2,1)}, u32[]{:S(2)}) copy-start(bf16[1024]{0:T(1024)(128)(2,1)} %param.8) | copy-start | bytes 6148
  0.0 43.0 %copy-start.3 = (bf16[1024,32]{0,1:T(8,128)(2,1)S(1)}, bf16[1024,32]{0,1:T(8,128)(2,1)}, u32[]{:S(2)}) copy-start(bf16[1024,32]{0,1:T(8,128)(2,1)} %param.10) | copy-start | bytes 196612
  0.0 43.0 %copy-start.2 = (bf16[256,1024]{1,0:T(8,128)(2,1)S(1)}, bf16[256,1024]{1,0:T(8,128)(2,1)}, u32[]{:S(2)}) copy-start(bf16[256,1024]{1,0:T(8,128)(2,1)} %param.7) | copy-start | bytes 1572868
  39.4 5.8 %collective-permute-start = (bf16[1024,512]{1,0:T(8,128)(2,1)S(1)}, bf16[1024,512]{1,0:T(8,128)(2,1)S(1)}, u32[]{:S(2)}, u32[]{:S(2)}) collective-permute-start(bf16[1024,512]{1,0:T(8,128)(2,1)S(1)} %bitcast.24), channel_id=1, source_target_pairs={{0,32},{32,0},{64,96},{96,64},{128,160},{160,128},{192,224},{224,1... | collective-permute-start | bytes 3145736 | tf_op jit(solution)/shard_map/ppermute | solution.py:112
  48.1 17.9 %copy-start.5 = (s32[1,4]{1,0:T(1,128)S(1)}, s32[1,4]{1,0:T(1,128)}, u32[]{:S(2)}) copy-start(s32[1,4]{1,0:T(1,128)} %param.12) | copy-start | bytes 52
  48.1 33.3 %all-to-all-start.1 = ((bf16[32,32,512]{2,1,0:T(8,128)(2,1)}), bf16[32,32,512]{2,1,0:T(8,128)(2,1)S(1)}, u32[]{:S(2)}, u32[]{:S(2)}) async-start(bf16[32,32,512]{2,1,0:T(8,128)(2,1)} %tile.5), calls=%async_computation.1 | async-start | bytes 2097152 | tf_op jit(solution)/shard_map/all_to_all | solution.py:109
  54.0 62.5 %collective-permute-start.6 = (bf16[2,2,256,1024]{3,2,1,0:T(8,128)(2,1)}, bf16[2,2,256,1024]{3,2,1,0:T(8,128)(2,1)}, u32[]{:S(2)}, u32[]{:S(2)}) collective-permute-start(bf16[2,2,256,1024]{3,2,1,0:T(8,128)(2,1)} %param.11), channel_id=1, source_target_pairs={{0,32},{1,33},{2,34},{3,35},{4,36},{5,37},{6,38},{7,39},{8,40},{9,... | collective-permute-start | bytes 6291464 | tf_op jit(solution)/shard_map/ppermute | solution.py:68
  58.0 58.5 %collective-permute-start.7 = (bf16[2,2,256,1024]{3,2,1,0:T(8,128)(2,1)}, bf16[2,2,256,1024]{3,2,1,0:T(8,128)(2,1)}, u32[]{:S(2)}, u32[]{:S(2)}) collective-permute-start(bf16[2,2,256,1024]{3,2,1,0:T(8,128)(2,1)} %param.11), channel_id=1, source_target_pairs={{32,0},{33,1},{34,2},{35,3},{36,4},{37,5},{38,6},{39,7},{40,8},{41... | collective-permute-start | bytes 6291464 | tf_op jit(solution)/shard_map/ppermute | solution.py:69
  61.0 0.7 collective-permute-start.1
  61.8 2.1 %collective-permute-start.3 = (bf16[2,2,32,1024]{3,2,1,0:T(8,128)(2,1)S(1)}, bf16[2,2,32,1024]{3,2,1,0:T(8,128)(2,1)S(1)}, u32[]{:S(2)}, u32[]{:S(2)}) collective-permute-start(bf16[2,2,32,1024]{3,2,1,0:T(8,128)(2,1)S(1)} %get-tuple-element.13), channel_id=1, source_target_pairs={{224,232},{225,233},{226,234},{227,235},{228,236},{229,237},{230,2... | collective-permute-start | bytes 786440 | tf_op jit(solution)/shard_map/ppermute | solution.py:87
  62.5 5.0 %collective-permute-start.2 = (bf16[2,2,64,1024]{3,2,1,0:T(8,128)(2,1)S(1)}, bf16[2,2,64,1024]{3,2,1,0:T(8,128)(2,1)S(1)}, u32[]{:S(2)}, u32[]{:S(2)}) collective-permute-start(bf16[2,2,64,1024]{3,2,1,0:T(8,128)(2,1)S(1)} %collective-permute-done.1), channel_id=1, source_target_pairs={{224,252},{225,253},{226,254},{227,255},{228,224},{229,225},{230,2... | collective-permute-start | bytes 1572872 | tf_op jit(solution)/shard_map/ppermute | solution.py:87
  63.2 4.3 %collective-permute-start.5 = (bf16[2,2,64,1024]{3,2,1,0:T(8,128)(2,1)S(1)}, bf16[2,2,64,1024]{3,2,1,0:T(8,128)(2,1)S(1)}, u32[]{:S(2)}, u32[]{:S(2)}) collective-permute-start(bf16[2,2,64,1024]{3,2,1,0:T(8,128)(2,1)S(1)} %collective-permute-done.1), channel_id=1, source_target_pairs={{224,228},{225,229},{226,230},{227,231},{228,232},{229,233},{230,2... | collective-permute-start | bytes 1572872 | tf_op jit(solution)/shard_map/ppermute | solution.py:87
  63.9 2.6 %collective-permute-start.4 = (bf16[2,2,32,1024]{3,2,1,0:T(8,128)(2,1)S(1)}, bf16[2,2,32,1024]{3,2,1,0:T(8,128)(2,1)}, u32[]{:S(2)}, u32[]{:S(2)}) collective-permute-start(bf16[2,2,32,1024]{3,2,1,0:T(8,128)(2,1)S(1)} %get-tuple-element.14), channel_id=1, source_target_pairs={{224,248},{225,249},{226,250},{227,251},{228,252},{229,253},{230,2... | collective-permute-start | bytes 786440 | tf_op jit(solution)/shard_map/ppermute | solution.py:87
  81.4 54.3 %collective-permute-start.8 = (bf16[1024,512]{1,0:T(8,128)(2,1)S(1)}, bf16[1024,512]{1,0:T(8,128)(2,1)}, u32[]{:S(2)}, u32[]{:S(2)}) collective-permute-start(bf16[1024,512]{1,0:T(8,128)(2,1)S(1)} %bitcast.23), channel_id=1, source_target_pairs={{0,32},{32,0},{64,96},{96,64},{128,160},{160,128},{192,224},{224,1... | collective-permute-start | bytes 3145736 | tf_op jit(solution)/shard_map/ppermute | solution.py:112
  135.7 1.4 %copy-start.1 = (bf16[256,1024]{1,0:T(8,128)(2,1)S(1)}, bf16[256,1024]{1,0:T(8,128)(2,1)}, u32[]{:S(2)}) copy-start(bf16[256,1024]{1,0:T(8,128)(2,1)} %shard_map.73) | copy-start | bytes 1572868
where the time goes:
time: 140 us; the launch traced here: 139 us
  starting transfers between devices  54 us (39%)
  blocking collectives  38.5 us (28%)
  other arithmetic  12.4 us (9%)
  waiting for transfers between devices  12 us (9%)
  Pallas kernels  12 us (9%)
  local copies, waits for them, and re-layouts  5.7 us (4%)
  matrix products  3.09 us (2%)
    all_to_all x1, blocking collectives, gathered_rows(): lax.all_to_all(jnp.tile(mine, (lon_count, 1)), 'lon', 0, 0, tiled=True)  38.5 us
    ppermute x2, starting transfers between devices, gathered_rows(): other = lax.ppermute(fetched, 'lat', swap)  38.1 us
    pallas_call x1, Pallas kernels, attend(): pl.pallas_call(attention_kernel, grid_spec=pltpu.PrefetchScalarGridSpec(n...  12 us
    all_to_all x1, waiting for transfers between devices, gathered_rows(): lax.all_to_all(jnp.tile(mine, (lon_count, 1)), 'lon', 0, 0, tiled=True)  9.97 us
    all_to_all x1, starting transfers between devices, gathered_rows(): lax.all_to_all(jnp.tile(mine, (lon_count, 1)), 'lon', 0, 0, tiled=True)  5.9 us
    concatenate x1, other arithmetic, layer(): window = jnp.concatenate([below, kv_cache, above], axis=1)  4.55 us
    ppermute x1, starting transfers between devices, neighbour_bands(): below = lax.ppermute(kv, both, up)  3.96 us
    ppermute x4, starting transfers between devices, along_z(): return lax.ppermute(value, both, pairs)  3.44 us
  transfers between devices with their start and end apart: 10, of which 2 were waited for; matrix products, arithmetic and copies ran while one was open for 10% of the time, Pallas kernels for 9%

commit v1 on v0

--- a/solution.py
+++ b/solution.py
@@ -61,7 +61,7 @@
 
 def neighbour_bands(kv):
     lat_count, lon_count = lax.axis_size("lat"), lax.axis_size("lon")
-    lat, lon = lax.axis_index("lat"), lax.axis_index("lon")
+    lon = lax.axis_index("lon")
     both = ("lat", "lon")
     split = lat_count // 2
     up = [(k * lon_count + l, (k + 1) * lon_count + l) for k in range(lat_count - 1) if k != split - 1 for l in range(lon_count)]
@@ -69,7 +69,6 @@
     above = lax.ppermute(kv, both, [(j, i) for i, j in up])
     rows = kv.shape[2] // Y_LO
     z = lon // Y_LO
-    z_count = lon_count // Y_LO
     piece = lax.dynamic_slice_in_dim(kv, (z % Y_LO) * rows, rows, axis=2)
     cross = []
     for l in range(lon_count):
@@ -77,6 +76,17 @@
         cross.append(((split - 1) * lon_count + l, split * lon_count + mirror))
         cross.append((split * lon_count + l, (split - 1) * lon_count + mirror))
     own = lax.ppermute(piece, both, cross)
+    return below, above, own
+
+
+def far_side(kv, below, above, own):
+    lat_count, lon_count = lax.axis_size("lat"), lax.axis_size("lon")
+    lat, lon = lax.axis_index("lat"), lax.axis_index("lon")
+    both = ("lat", "lon")
+    split = lat_count // 2
+    rows = kv.shape[2] // Y_LO
+    z = lon // Y_LO
+    z_count = lon_count // Y_LO
 
     def along_z(value, shift):
         pairs = []
@@ -119,18 +129,19 @@
     rows = queries.astype(jnp.float32)
     rowwise_scale = lax.rsqrt(jnp.mean(rows * rows, axis=1, keepdims=True) + 1e-05)
     normed = (rows * rowwise_scale * gain.astype(jnp.float32)[None, :]).astype(jnp.bfloat16)
-    w_query_rows = gathered_rows(w_query)
+    blocks_here = kv_cache.shape[1]
+    sent = neighbour_bands(kv_cache)
+    w_query_rows = gathered_rows(w_query, after=sent[2])
     projected = jnp.dot(
         normed,
         w_query_rows,
         preferred_element_type=jnp.float32,
     )
     query = (projected * HD ** (-0.5)).astype(jnp.bfloat16)
-    blocks_here = kv_cache.shape[1]
-    below, above = neighbour_bands(kv_cache)
+    local_lists = nbr_lists - (lax.axis_index("lat") - 1) * blocks_here
+    slots = jnp.clip(local_lists[0], 0, 3 * blocks_here - 1)
+    below, above = far_side(kv_cache, *sent)
     window = jnp.concatenate([below, kv_cache, above], axis=1)
-    local_lists = nbr_lists - (lax.axis_index("lat") - 1) * blocks_here
-    slots = jnp.clip(local_lists[0], 0, window.shape[1] - 1)
     attended = attend(query, window, slots, counts)
     w_out_rows = gathered_rows(w_out.T, after=query)
     decoded = lax.dot_general(

time: 140 us -> 143 us (1.021)
  the two profiles are of different devices: /device:TPU:41 before, /device:TPU:57 now
where the time goes in v1:
time: 143 us; the launch traced here: 142 us
  starting transfers between devices  62 us (43%)
  blocking collectives  30 us (21%)
  waiting for transfers between devices  16.3 us (11%)
  other arithmetic  12.4 us (9%)
  Pallas kernels  12 us (8%)
  local copies, waits for them, and re-layouts  4.97 us (3%)
  matrix products  3.09 us (2%)
    ppermute x2, starting transfers between devices, gathered_rows(): other = lax.ppermute(fetched, 'lat', swap)  47.1 us
    all_to_all x1, blocking collectives, gathered_rows(): lax.all_to_all(jnp.tile(mine, (lon_count, 1)), 'lon', 0, 0, tiled=True)  30 us
    all_to_all x1, waiting for transfers between devices, gathered_rows(): lax.all_to_all(jnp.tile(mine, (lon_count, 1)), 'lon', 0, 0, tiled=True)  14.3 us
    pallas_call x1, Pallas kernels, attend(): pl.pallas_call(attention_kernel, grid_spec=pltpu.PrefetchScalarGridSpec(n...  12 us
    all_to_all x1, starting transfers between devices, gathered_rows(): lax.all_to_all(jnp.tile(mine, (lon_count, 1)), 'lon', 0, 0, tiled=True)  5.11 us
    concatenate x1, other arithmetic, layer(): window = jnp.concatenate([below, kv_cache, above], axis=1)  4.55 us
    ppermute x1, starting transfers between devices, neighbour_bands(): above = lax.ppermute(kv, both, [(j, i) for i, j in up])  3.73 us
    ppermute x4, starting transfers between devices, along_z(): return lax.ppermute(value, both, pairs)  3.44 us
  transfers between devices with their start and end apart: 10, of which 2 were waited for; matrix products, arithmetic and copies ran while one was open for 9% of the time, Pallas kernels for 8%

profile of v1, /device:TPU:57, one launch (start us, length us, event | category | flops | bytes accessed | tf_op | source)
XLA Modules:
  0.0 141.8 jit_solution(11651834257735202617)
XLA Ops:
  0.0 0.0 copy-start
  0.0 0.0 copy-start.4
  0.0 0.0 copy-start.3
  0.0 0.0 copy-start.2
  0.0 1.1 constant_dynamic-slice_fusion
  1.2 0.7 collective-permute-start
  1.9 0.0 copy-done
  1.9 0.0 collective-permute-done
  1.9 0.1 tile.4
  2.0 30.0 %all_to_all.18 = bf16[32,32,512]{2,1,0:T(8,128)(2,1)S(1)} all-to-all(bf16[32,32,512]{2,1,0:T(8,128)(2,1)S(1)} %tile.4), channel_id=1, replica_groups=mesh['lat'=16,'lon'=32] {'lon'}, dimensions={0} | all-to-all | bytes 2097152 | tf_op jit(solution)/shard_map/all_to_all | solution.py:119
  32.1 26.2 %collective-permute-start.1 = (bf16[1024,512]{1,0:T(8,128)(2,1)S(1)}, bf16[1024,512]{1,0:T(8,128)(2,1)S(1)}, u32[]{:S(2)}, u32[]{:S(2)}) collective-permute-start(bf16[1024,512]{1,0:T(8,128)(2,1)S(1)} %bitcast.24), channel_id=1, source_target_pairs={{0,32},{32,0},{64,96},{96,64},{128,160},{160,128},{192,224},{224,1... | collective-permute-start | bytes 3145736 | tf_op jit(solution)/shard_map/ppermute | solution.py:122
  58.3 0.0 copy-done.4
  58.3 0.0 copy-done.3
  58.3 0.0 copy-done.2
  58.3 0.2 fusion.17
  58.5 2.0 %collective-permute-done.1 = bf16[1024,512]{1,0:T(8,128)(2,1)S(1)} collective-permute-done((bf16[1024,512]{1,0:T(8,128)(2,1)S(1)}, bf16[1024,512]{1,0:T(8,128)(2,1)S(1)}, u32[]{:S(2)}, u32[]{:S(2)}) %collective-permute-start.1) | collective-permute-done | bytes 1048608 | tf_op jit(solution)/shard_map/ppermute | solution.py:122
  60.5 0.2 broadcast_select_fusion.3
  60.7 1.6 %fusion.11.q_ref = bf16[256,1024]{1,0:T(8,128)(2,1)} fusion(bf16[1024,512]{1,0:T(8,128)(2,1)S(1)} %get-tuple-element.14, bf16[1024,512]{1,0:T(8,128)(2,1)S(1)} %get-tuple-element.13, bf16[256,1024]{1,0:T(8,128)(2,1)S(1)} %copy-done.2, f32[1024]{0:T(1024)S(1)} %convert_element_type.16, f32[256]{0:T(256)S(1)} %add_rsqrt_fusion), kind=kOutput, calls=%fused_computation.17 | convolution fusion | flops 542638080 | bytes 3150848 | tf_op jit(solution)/shard_map/dot_general | solution.py:135
  62.3 1.1 tile.5
  63.4 5.1 %all-to-all-start.1 = ((bf16[32,32,512]{2,1,0:T(8,128)(2,1)}), bf16[32,32,512]{2,1,0:T(8,128)(2,1)S(1)}, u32[]{:S(2)}, u32[]{:S(2)}) async-start(bf16[32,32,512]{2,1,0:T(8,128)(2,1)} %tile.5), calls=%async_computation.1 | async-start | bytes 2097152 | tf_op jit(solution)/shard_map/all_to_all | solution.py:119
  68.5 1.9 %collective-permute-start.6 = (bf16[2,2,256,1024]{3,2,1,0:T(8,128)(2,1)}, bf16[2,2,256,1024]{3,2,1,0:T(8,128)(2,1)}, u32[]{:S(2)}, u32[]{:S(2)}) collective-permute-start(bf16[2,2,256,1024]{3,2,1,0:T(8,128)(2,1)} %param.11), channel_id=1, source_target_pairs={{0,32},{1,33},{2,34},{3,35},{4,36},{5,37},{6,38},{7,39},{8,40},{9,... | collective-permute-start | bytes 6291464 | tf_op jit(solution)/shard_map/ppermute | solution.py:68
  70.5 3.7 %collective-permute-start.7 = (bf16[2,2,256,1024]{3,2,1,0:T(8,128)(2,1)}, bf16[2,2,256,1024]{3,2,1,0:T(8,128)(2,1)}, u32[]{:S(2)}, u32[]{:S(2)}) collective-permute-start(bf16[2,2,256,1024]{3,2,1,0:T(8,128)(2,1)} %param.11), channel_id=1, source_target_pairs={{32,0},{33,1},{34,2},{35,3},{36,4},{37,5},{38,6},{39,7},{40,8},{41... | collective-permute-start | bytes 6291464 | tf_op jit(solution)/shard_map/ppermute | solution.py:69
  74.2 0.7 collective-permute-start.3
  74.9 0.7 collective-permute-start.2
  75.6 0.7 collective-permute-start.5
  76.4 0.0 collective-permute-done.3
  76.4 1.4 collective-permute-start.4
  78.4 0.0 copy-done.5
  78.4 0.5 clamp_bitcast_fusion.slots_ref
  78.9 0.0 collective-permute-done.4
  78.9 1.0 maximum_bitcast_fusion
  79.9 0.0 collective-permute-done.2
  79.9 0.0 collective-permute-done.5
  80.0 1.6 %pad_maximum_fusion.1 = bf16[4,2,2,64,1024]{4,3,2,1,0:T(8,128)(2,1)} fusion(bf16[1,2,2,64,1024]{4,3,2,1,0:T(8,128)(2,1)S(1)} %bitcast.27, bf16[1,2,2,64,1024]{4,3,2,1,0:T(8,128)(2,1)S(1)} %maximum_bitcast_fusion, bf16[1,2,2,64,1024]{4,3,2,1,0:T(8,128)(2,1)S(1)} %bitcast.26, bf16[1,2,2,64,1024]{4,3,2,1,0:T(8,128)(2,1)S(1)} %bitcast.25), kind=kLoop, calls=%fused_computation.6 | loop fusion | flops 3145728 | bytes 4194304 | tf_op jit(solution)/shard_map/stack | solution.py:103
  81.6 2.3 %gather_fusion = bf16[4,2,2,64,1024]{4,3,2,1,0:T(8,128)(2,1)S(1)} fusion(bf16[4,2,2,64,1024]{4,3,2,1,0:T(8,128)(2,1)} %pad_maximum_fusion.1, s32[1024]{0:T(1024)S(1)} %pad_clamp_fusion), kind=kCustom, calls=%fused_computation | custom fusion | bytes 4194320 | tf_op jit(solution)/shard_map/jit(_take)/gather | solution.py:105
  83.9 14.3 %all-to-all-done.1 = bf16[32,32,512]{2,1,0:T(8,128)(2,1)S(1)} async-done(((bf16[32,32,512]{2,1,0:T(8,128)(2,1)}), bf16[32,32,512]{2,1,0:T(8,128)(2,1)S(1)}, u32[]{:S(2)}, u32[]{:S(2)}) %all-to-all-start.1) | async-done | bytes 1048608 | tf_op jit(solution)/shard_map/all_to_all | solution.py:119
  98.2 20.9 %collective-permute-start.8 = (bf16[1024,512]{1,0:T(8,128)(2,1)S(1)}, bf16[1024,512]{1,0:T(8,128)(2,1)}, u32[]{:S(2)}, u32[]{:S(2)}) collective-permute-start(bf16[1024,512]{1,0:T(8,128)(2,1)S(1)} %bitcast.23), channel_id=1, source_target_pairs={{0,32},{32,0},{64,96},{96,64},{128,160},{160,128},{192,224},{224,1... | collective-permute-start | bytes 3145736 | tf_op jit(solution)/shard_map/ppermute | solution.py:122
  119.0 0.3 select_bitcast_fusion
  119.3 0.3 copy.8
  119.6 0.0 collective-permute-done.6
  119.6 0.0 collective-permute-done.7
  119.6 2.6 %bitcast_select_fusion.1 = (bf16[2,2,256,1024]{3,2,1,0:T(8,128)(2,1)S(1)}, bf16[2,2,256,1024]{3,2,1,0:T(8,128)(2,1)S(1)}) fusion(bf16[2,2,256,1024]{3,2,1,0:T(8,128)(2,1)} %collective-permute-done.6, bf16[2,2,4,64,1024]{4,3,2,1,0:T(8,128)(2,1)S(1)} %copy.8, pred[]{:T(512)S(6)} %eq.19, bf16[2,2,256,1024]{3,2,1,0:T(8,128)(2,1)} %collective-permute-done.7, ...), kind=kLoop, calls=%fused_computation.12 | loop fusion | flops 2097152 | bytes 10485762 | tf_op jit(solution)/shard_map/jit(_where)/select_n | solution.py:107
  122.2 4.5 %pad_maximum_fusion.refs_0_.refs_1_.refs_2_.refs_3_.refs_4_.refs_5_.refs_6_.refs_7_ = bf16[2,6,256,1024]{3,2,1,0:T(8,128)(2,1)} fusion(bf16[2,2,256,1024]{3,2,1,0:T(8,128)(2,1)S(1)} %get-tuple-element.12, bf16[2,2,256,1024]{3,2,1,0:T(8,128)(2,1)} %param.11, bf16[2,2,256,1024]{3,2,1,0:T(8,128)(2,1)S(1)} %get-tuple-element.11), kind=kLoop, calls=%fused_computation.1 | loop fusion | flops 6291456 | bytes 12582912 | tf_op jit(solution)/shard_map/concatenate | solution.py:144
  126.7 12.0 %shard_map.73 = bf16[256,1024]{1,0:T(8,128)(2,1)} custom-call(s32[4]{0:T(128)} %clamp_bitcast_fusion.slots_ref, s32[1]{0:T(128)S(6)} %copy.9.count_ref, bf16[256,1024]{1,0:T(8,128)(2,1)} %fusion.11.q_ref, bf16[2,6,256,1024]{3,2,1,0:T(8,128)(2,1)} %pad_maximum_fusion.refs_0_.refs_1_.refs_2_.refs_3_.refs_4_.refs_5_.refs_6_.refs_7_, ...), custom_call_target="tpu_custom_call" | custom-call | tf_op jit(solution)/shard_map/pallas_call | solution.py:51
  138.8 0.0 collective-permute-done.8
  138.8 1.4 %broadcast_select_fusion.1 = (bf16[1024,512]{1,0:T(8,128)(2,1)S(1)}, bf16[1024,512]{1,0:T(8,128)(2,1)S(1)}) fusion(bf16[1024,512]{1,0:T(8,128)(2,1)} %collective-permute-done.8, pred[]{:T(512)S(6)} %eq.18, bf16[32,32,512]{2,1,0:T(8,128)(2,1)S(1)} %all-to-all-done.1), kind=kLoop, calls=%fused_computation.23 | loop fusion | flops 1048576 | bytes 4194305 | tf_op jit(solution)/shard_map/jit(_where)/select_n | solution.py:123
  140.2 0.0 copy-done.1
  140.2 1.5 %fusion.14 = bf16[256,1024]{1,0:T(8,128)(2,1)} fusion(bf16[256,1024]{1,0:T(8,128)(2,1)S(1)} %copy-done.1, bf16[1024,512]{1,0:T(8,128)(2,1)S(1)} %get-tuple-element.10, bf16[1024,512]{1,0:T(8,128)(2,1)S(1)} %get-tuple-element.9), kind=kOutput, calls=%fused_computation.18 | convolution fusion | flops 541327360 | bytes 3145728 | tf_op jit(solution)/shard_map/dot_general | solution.py:147
  (10 shorter events, 0.1 us)
Async XLA Ops:
  0.0 1.9 %copy-start = (bf16[32,1024]{1,0:T(8,128)(2,1)S(1)}, bf16[32,1024]{1,0:T(8,128)(2,1)}, u32[]{:S(2)}) copy-start(bf16[32,1024]{1,0:T(8,128)(2,1)} %param.9) | copy-start | bytes 196612
  0.0 58.3 %copy-start.4 = (bf16[1024]{0:T(1024)(128)(2,1)S(1)}, bf16[1024]{0:T(1024)(128)(2,1)}, u32[]{:S(2)}) copy-start(bf16[1024]{0:T(1024)(128)(2,1)} %param.8) | copy-start | bytes 6148
  0.0 58.3 %copy-start.3 = (bf16[1024,32]{0,1:T(8,128)(2,1)S(1)}, bf16[1024,32]{0,1:T(8,128)(2,1)}, u32[]{:S(2)}) copy-start(bf16[1024,32]{0,1:T(8,128)(2,1)} %param.10) | copy-start | bytes 196612
  0.0 58.3 %copy-start.2 = (bf16[256,1024]{1,0:T(8,128)(2,1)S(1)}, bf16[256,1024]{1,0:T(8,128)(2,1)}, u32[]{:S(2)}) copy-start(bf16[256,1024]{1,0:T(8,128)(2,1)} %param.7) | copy-start | bytes 1572868
  1.2 0.8 collective-permute-start
  32.1 28.5 %collective-permute-start.1 = (bf16[1024,512]{1,0:T(8,128)(2,1)S(1)}, bf16[1024,512]{1,0:T(8,128)(2,1)S(1)}, u32[]{:S(2)}, u32[]{:S(2)}) collective-permute-start(bf16[1024,512]{1,0:T(8,128)(2,1)S(1)} %bitcast.24), channel_id=1, source_target_pairs={{0,32},{32,0},{64,96},{96,64},{128,160},{160,128},{192,224},{224,1... | collective-permute-start | bytes 3145736 | tf_op jit(solution)/shard_map/ppermute | solution.py:122
  62.3 16.1 %copy-start.5 = (s32[1,4]{1,0:T(1,128)S(1)}, s32[1,4]{1,0:T(1,128)}, u32[]{:S(2)}) copy-start(s32[1,4]{1,0:T(1,128)} %param.12) | copy-start | bytes 52
  63.4 34.8 %all-to-all-start.1 = ((bf16[32,32,512]{2,1,0:T(8,128)(2,1)}), bf16[32,32,512]{2,1,0:T(8,128)(2,1)S(1)}, u32[]{:S(2)}, u32[]{:S(2)}) async-start(bf16[32,32,512]{2,1,0:T(8,128)(2,1)} %tile.5), calls=%async_computation.1 | async-start | bytes 2097152 | tf_op jit(solution)/shard_map/all_to_all | solution.py:119
  68.5 51.0 %collective-permute-start.6 = (bf16[2,2,256,1024]{3,2,1,0:T(8,128)(2,1)}, bf16[2,2,256,1024]{3,2,1,0:T(8,128)(2,1)}, u32[]{:S(2)}, u32[]{:S(2)}) collective-permute-start(bf16[2,2,256,1024]{3,2,1,0:T(8,128)(2,1)} %param.11), channel_id=1, source_target_pairs={{0,32},{1,33},{2,34},{3,35},{4,36},{5,37},{6,38},{7,39},{8,40},{9,... | collective-permute-start | bytes 6291464 | tf_op jit(solution)/shard_map/ppermute | solution.py:68
  70.5 49.1 %collective-permute-start.7 = (bf16[2,2,256,1024]{3,2,1,0:T(8,128)(2,1)}, bf16[2,2,256,1024]{3,2,1,0:T(8,128)(2,1)}, u32[]{:S(2)}, u32[]{:S(2)}) collective-permute-start(bf16[2,2,256,1024]{3,2,1,0:T(8,128)(2,1)} %param.11), channel_id=1, source_target_pairs={{32,0},{33,1},{34,2},{35,3},{36,4},{37,5},{38,6},{39,7},{40,8},{41... | collective-permute-start | bytes 6291464 | tf_op jit(solution)/shard_map/ppermute | solution.py:69
  74.2 2.1 %collective-permute-start.3 = (bf16[2,2,32,1024]{3,2,1,0:T(8,128)(2,1)S(1)}, bf16[2,2,32,1024]{3,2,1,0:T(8,128)(2,1)S(1)}, u32[]{:S(2)}, u32[]{:S(2)}) collective-permute-start(bf16[2,2,32,1024]{3,2,1,0:T(8,128)(2,1)S(1)} %get-tuple-element.15), channel_id=1, source_target_pairs={{224,232},{225,233},{226,234},{227,235},{228,236},{229,237},{230,2... | collective-permute-start | bytes 786440 | tf_op jit(solution)/shard_map/ppermute | solution.py:97
  74.9 5.0 %collective-permute-start.2 = (bf16[2,2,64,1024]{3,2,1,0:T(8,128)(2,1)S(1)}, bf16[2,2,64,1024]{3,2,1,0:T(8,128)(2,1)S(1)}, u32[]{:S(2)}, u32[]{:S(2)}) collective-permute-start(bf16[2,2,64,1024]{3,2,1,0:T(8,128)(2,1)S(1)} %collective-permute-done), channel_id=1, source_target_pairs={{224,252},{225,253},{226,254},{227,255},{228,224},{229,225},{230,2... | collective-permute-start | bytes 1572872 | tf_op jit(solution)/shard_map/ppermute | solution.py:97
  75.6 4.3 %collective-permute-start.5 = (bf16[2,2,64,1024]{3,2,1,0:T(8,128)(2,1)S(1)}, bf16[2,2,64,1024]{3,2,1,0:T(8,128)(2,1)S(1)}, u32[]{:S(2)}, u32[]{:S(2)}) collective-permute-start(bf16[2,2,64,1024]{3,2,1,0:T(8,128)(2,1)S(1)} %collective-permute-done), channel_id=1, source_target_pairs={{224,228},{225,229},{226,230},{227,231},{228,232},{229,233},{230,2... | collective-permute-start | bytes 1572872 | tf_op jit(solution)/shard_map/ppermute | solution.py:97
  76.4 2.6 %collective-permute-start.4 = (bf16[2,2,32,1024]{3,2,1,0:T(8,128)(2,1)S(1)}, bf16[2,2,32,1024]{3,2,1,0:T(8,128)(2,1)}, u32[]{:S(2)}, u32[]{:S(2)}) collective-permute-start(bf16[2,2,32,1024]{3,2,1,0:T(8,128)(2,1)S(1)} %get-tuple-element.16), channel_id=1, source_target_pairs={{224,248},{225,249},{226,250},{227,251},{228,252},{229,253},{230,2... | collective-permute-start | bytes 786440 | tf_op jit(solution)/shard_map/ppermute | solution.py:97
  98.2 40.6 %collective-permute-start.8 = (bf16[1024,512]{1,0:T(8,128)(2,1)S(1)}, bf16[1024,512]{1,0:T(8,128)(2,1)}, u32[]{:S(2)}, u32[]{:S(2)}) collective-permute-start(bf16[1024,512]{1,0:T(8,128)(2,1)S(1)} %bitcast.23), channel_id=1, source_target_pairs={{0,32},{32,0},{64,96},{96,64},{128,160},{160,128},{192,224},{224,1... | collective-permute-start | bytes 3145736 | tf_op jit(solution)/shard_map/ppermute | solution.py:122
  138.8 1.4 %copy-start.1 = (bf16[256,1024]{1,0:T(8,128)(2,1)S(1)}, bf16[256,1024]{1,0:T(8,128)(2,1)}, u32[]{:S(2)}) copy-start(bf16[256,1024]{1,0:T(8,128)(2,1)} %shard_map.73) | copy-start | bytes 1572868

commit v2 on v1

--- a/solution.py
+++ b/solution.py
@@ -22,7 +22,7 @@
         scores = []
         for slot, key_ref in enumerate(key_refs):
             s = lax.dot_general(q_head, key_ref[...], (((1,), (1,)), ((), ())), preferred_element_type=jnp.float32)
-            scores.append(jnp.where(slot < count, s, -jnp.inf))
+            scores.append(s if slot == 0 else jnp.where(slot < count, s, -jnp.inf))
         peak = scores[0].max(axis=1, keepdims=True)
         for s in scores[1:]:
             peak = jnp.maximum(peak, s.max(axis=1, keepdims=True))
@@ -79,13 +79,10 @@
     return below, above, own
 
 
-def far_side(kv, below, above, own):
+def far_side(own):
     lat_count, lon_count = lax.axis_size("lat"), lax.axis_size("lon")
-    lat, lon = lax.axis_index("lat"), lax.axis_index("lon")
     both = ("lat", "lon")
     split = lat_count // 2
-    rows = kv.shape[2] // Y_LO
-    z = lon // Y_LO
     z_count = lon_count // Y_LO
 
     def along_z(value, shift):
@@ -96,17 +93,16 @@
                 pairs.append((band * lon_count + l, band * lon_count + target))
         return lax.ppermute(value, both, pairs)
 
-    half = rows // 2
-    opposite = jnp.concatenate(
-        [along_z(own[:, :, :half], 2), along_z(own[:, :, half:], -2)], axis=2
-    )
-    quarters = jnp.stack([own, along_z(own, -1), opposite, along_z(own, 1)])
+    moved = [along_z(own, 2), along_z(own, -1), along_z(own, 1)]
+    return moved
+
+
+def assembled(kv, own, moved):
+    z = lax.axis_index("lon") // Y_LO
+    quarters = jnp.stack([own, moved[1], moved[0], moved[2]])
     order = (jnp.arange(Y_LO) - z) % Y_LO
     joined = jnp.take(quarters, order, axis=0)
-    joined = jnp.moveaxis(joined, 0, 2).reshape(kv.shape)
-    below = jnp.where(lat == split, joined, below)
-    above = jnp.where(lat == split - 1, joined, above)
-    return below, above
+    return jnp.moveaxis(joined, 0, 2).reshape(kv.shape)
 
 
 def gathered_rows(local, after=None):
@@ -138,10 +134,17 @@
         preferred_element_type=jnp.float32,
     )
     query = (projected * HD ** (-0.5)).astype(jnp.bfloat16)
-    local_lists = nbr_lists - (lax.axis_index("lat") - 1) * blocks_here
-    slots = jnp.clip(local_lists[0], 0, 3 * blocks_here - 1)
-    below, above = far_side(kv_cache, *sent)
-    window = jnp.concatenate([below, kv_cache, above], axis=1)
+    lat = lax.axis_index("lat")
+    split = lax.axis_size("lat") // 2
+    local_lists = jnp.clip(nbr_lists[0] - (lat - 1) * blocks_here, 0, 3 * blocks_here - 1)
+    crossing = ((lat == split) & (local_lists < blocks_here)) | (
+        (lat == split - 1) & (local_lists >= 2 * blocks_here)
+    )
+    slots = jnp.where(crossing, 3 * blocks_here + local_lists % blocks_here, local_lists)
+    moved = far_side(sent[2])
+    below, above, own = sent
+    joined = assembled(kv_cache, own, moved)
+    window = jnp.concatenate([below, kv_cache, above, joined], axis=1)
     attended = attend(query, window, slots, counts)
     w_out_rows = gathered_rows(w_out.T, after=query)
     decoded = lax.dot_general(

time: 143 us -> 140 us (0.979)
  the two profiles are of different devices: /device:TPU:57 before, /device:TPU:6 now
where the time goes in v2:
time: 140 us; the launch traced here: 139 us
  starting transfers between devices  53.4 us (38%)
  blocking collectives  31.7 us (23%)
  waiting for transfers between devices  21 us (15%)
  Pallas kernels  12 us (9%)
  other arithmetic  11 us (8%)
  local copies, waits for them, and re-layouts  5.61 us (4%)
  matrix products  3.08 us (2%)
    ppermute x2, starting transfers between devices, gathered_rows(): other = lax.ppermute(fetched, 'lat', swap)  39.5 us
    all_to_all x1, blocking collectives, gathered_rows(): lax.all_to_all(jnp.tile(mine, (lon_count, 1)), 'lon', 0, 0, tiled=True)  31.7 us
    all_to_all x1, waiting for transfers between devices, gathered_rows(): lax.all_to_all(jnp.tile(mine, (lon_count, 1)), 'lon', 0, 0, tiled=True)  18.9 us
    pallas_call x1, Pallas kernels, attend(): pl.pallas_call(attention_kernel, grid_spec=pltpu.PrefetchScalarGridSpec(n...  12 us
    concatenate x1, other arithmetic, layer(): window = jnp.concatenate([below, kv_cache, above, joined], axis=1)  6.67 us
    all_to_all x1, starting transfers between devices, gathered_rows(): lax.all_to_all(jnp.tile(mine, (lon_count, 1)), 'lon', 0, 0, tiled=True)  5.53 us
    ppermute x1, starting transfers between devices, neighbour_bands(): above = lax.ppermute(kv, both, [(j, i) for i, j in up])  3.58 us
  transfers between devices with their start and end apart: 9, of which 2 were waited for; matrix products, arithmetic and copies ran while one was open for 9% of the time, Pallas kernels for 9%

profile of v2, /device:TPU:6, one launch (start us, length us, event | category | flops | bytes accessed | tf_op | source)
XLA Modules:
  0.0 138.7 jit_solution(3237135825349328409)
XLA Ops:
  0.0 0.0 copy-start
  0.0 0.0 copy-start.6
  0.0 0.0 copy-start.5
  0.0 0.0 copy-start.2
  0.0 1.1 constant_dynamic-slice_fusion
  1.2 0.7 collective-permute-start
  1.9 0.0 copy-done
  1.9 0.0 collective-permute-done
  1.9 0.0 copy-start.3
  1.9 0.8 copy-done.3
  2.7 0.1 tile.4
  2.8 31.7 %all_to_all.18 = bf16[32,32,512]{2,1,0:T(8,128)(2,1)S(1)} all-to-all(bf16[32,32,512]{2,1,0:T(8,128)(2,1)S(1)} %tile.4), channel_id=1, replica_groups=mesh['lat'=16,'lon'=32] {'lon'}, dimensions={0} | all-to-all | bytes 2097152 | tf_op jit(solution)/shard_map/all_to_all | solution.py:115
  34.5 22.6 %collective-permute-start.1 = (bf16[1024,512]{1,0:T(8,128)(2,1)S(1)}, bf16[1024,512]{1,0:T(8,128)(2,1)S(1)}, u32[]{:S(2)}, u32[]{:S(2)}) collective-permute-start(bf16[1024,512]{1,0:T(8,128)(2,1)S(1)} %bitcast.22), channel_id=1, source_target_pairs={{0,32},{32,0},{64,96},{96,64},{128,160},{160,128},{192,224},{224,1... | collective-permute-start | bytes 3145736 | tf_op jit(solution)/shard_map/ppermute | solution.py:118
  57.1 0.0 copy-done.6
  57.2 0.0 copy-done.5
  57.2 0.0 copy-done.2
  57.2 0.2 fusion.17
  57.4 2.0 %collective-permute-done.1 = bf16[1024,512]{1,0:T(8,128)(2,1)S(1)} collective-permute-done((bf16[1024,512]{1,0:T(8,128)(2,1)S(1)}, bf16[1024,512]{1,0:T(8,128)(2,1)S(1)}, u32[]{:S(2)}, u32[]{:S(2)}) %collective-permute-start.1) | collective-permute-done | bytes 1048608 | tf_op jit(solution)/shard_map/ppermute | solution.py:118
  59.4 0.2 broadcast_select_fusion.3
  59.6 1.5 %fusion.11.q_ref = bf16[256,1024]{1,0:T(8,128)(2,1)} fusion(bf16[1024,512]{1,0:T(8,128)(2,1)S(1)} %get-tuple-element.12, bf16[1024,512]{1,0:T(8,128)(2,1)S(1)} %get-tuple-element.11, bf16[256,1024]{1,0:T(8,128)(2,1)S(1)} %copy-done.2, f32[1024]{0:T(1024)S(1)} %convert_element_type.16, f32[256]{0:T(256)S(1)} %add_rsqrt_fusion), kind=kOutput, calls=%fused_computation.15 | convolution fusion | flops 542638080 | bytes 3150848 | tf_op jit(solution)/shard_map/dot_general | solution.py:131
  61.1 0.0 copy-start.4
  61.2 1.1 tile.5
  62.2 5.5 %all-to-all-start.1 = ((bf16[32,32,512]{2,1,0:T(8,128)(2,1)}), bf16[32,32,512]{2,1,0:T(8,128)(2,1)S(1)}, u32[]{:S(2)}, u32[]{:S(2)}) async-start(bf16[32,32,512]{2,1,0:T(8,128)(2,1)} %tile.5), calls=%async_computation.1 | async-start | bytes 2097152 | tf_op jit(solution)/shard_map/all_to_all | solution.py:115
  67.8 2.0 %collective-permute-start.2 = (bf16[2,2,256,1024]{3,2,1,0:T(8,128)(2,1)}, bf16[2,2,256,1024]{3,2,1,0:T(8,128)(2,1)}, u32[]{:S(2)}, u32[]{:S(2)}) collective-permute-start(bf16[2,2,256,1024]{3,2,1,0:T(8,128)(2,1)} %param.11), channel_id=1, source_target_pairs={{0,32},{1,33},{2,34},{3,35},{4,36},{5,37},{6,38},{7,39},{8,40},{9,... | collective-permute-start | bytes 6291464 | tf_op jit(solution)/shard_map/ppermute | solution.py:68
  69.8 3.6 %collective-permute-start.3 = (bf16[2,2,256,1024]{3,2,1,0:T(8,128)(2,1)}, bf16[2,2,256,1024]{3,2,1,0:T(8,128)(2,1)}, u32[]{:S(2)}, u32[]{:S(2)}) collective-permute-start(bf16[2,2,256,1024]{3,2,1,0:T(8,128)(2,1)} %param.11), channel_id=1, source_target_pairs={{32,0},{33,1},{34,2},{35,3},{36,4},{37,5},{38,6},{39,7},{40,8},{41... | collective-permute-start | bytes 6291464 | tf_op jit(solution)/shard_map/ppermute | solution.py:69
  74.0 0.0 copy-done.4
  74.0 0.7 collective-permute-start.4
  74.7 0.7 collective-permute-start.5
  75.4 0.7 collective-permute-start.6
  76.2 0.0 copy-done.7
  76.2 0.6 or_select_fusion.slots_ref
  76.8 0.0 collective-permute-done.4
  76.8 0.0 collective-permute-done.5
  76.8 0.0 collective-permute-done.6
  76.8 1.6 %pad_maximum_fusion.1 = bf16[4,2,2,64,1024]{4,3,2,1,0:T(8,128)(2,1)} fusion(bf16[1,2,2,64,1024]{4,3,2,1,0:T(8,128)(2,1)S(1)} %bitcast.26, bf16[1,2,2,64,1024]{4,3,2,1,0:T(8,128)(2,1)S(1)} %bitcast.25, bf16[1,2,2,64,1024]{4,3,2,1,0:T(8,128)(2,1)S(1)} %bitcast.24, bf16[1,2,2,64,1024]{4,3,2,1,0:T(8,128)(2,1)S(1)} %bitcast.23), kind=kLoop, calls=%fused_computation.6 | loop fusion | flops 3145728 | bytes 4194304 | tf_op jit(solution)/shard_map/stack | solution.py:102
  78.4 2.3 %gather_fusion = bf16[4,2,2,64,1024]{4,3,2,1,0:T(8,128)(2,1)S(1)} fusion(bf16[4,2,2,64,1024]{4,3,2,1,0:T(8,128)(2,1)} %pad_maximum_fusion.1, s32[1024]{0:T(1024)S(1)} %pad_clamp_fusion), kind=kCustom, calls=%fused_computation | custom fusion | bytes 4194320 | tf_op jit(solution)/shard_map/jit(_take)/gather | solution.py:104
  80.7 18.9 %all-to-all-done.1 = bf16[32,32,512]{2,1,0:T(8,128)(2,1)S(1)} async-done(((bf16[32,32,512]{2,1,0:T(8,128)(2,1)}), bf16[32,32,512]{2,1,0:T(8,128)(2,1)S(1)}, u32[]{:S(2)}, u32[]{:S(2)}) %all-to-all-start.1) | async-done | bytes 1048608 | tf_op jit(solution)/shard_map/all_to_all | solution.py:115
  99.6 16.9 %collective-permute-start.7 = (bf16[1024,512]{1,0:T(8,128)(2,1)S(1)}, bf16[1024,512]{1,0:T(8,128)(2,1)}, u32[]{:S(2)}, u32[]{:S(2)}) collective-permute-start(bf16[1024,512]{1,0:T(8,128)(2,1)S(1)} %bitcast.21), channel_id=1, source_target_pairs={{0,32},{32,0},{64,96},{96,64},{128,160},{160,128},{192,224},{224,1... | collective-permute-start | bytes 3145736 | tf_op jit(solution)/shard_map/ppermute | solution.py:118
  116.5 0.3 select_bitcast_fusion
  116.8 0.2 copy.8
  117.0 0.0 collective-permute-done.2
  117.0 0.0 collective-permute-done.3
  117.0 6.7 %pad_maximum_fusion.refs_0_.refs_1_.refs_2_.refs_3_.refs_4_.refs_5_.refs_6_.refs_7_ = bf16[2,8,256,1024]{3,2,1,0:T(8,128)(2,1)} fusion(bf16[2,2,256,1024]{3,2,1,0:T(8,128)(2,1)S(1)} %bitcast.20, bf16[2,2,256,1024]{3,2,1,0:T(8,128)(2,1)} %collective-permute-done.3, bf16[2,2,256,1024]{3,2,1,0:T(8,128)(2,1)} %param.11, ...), kind=kLoop, calls=%fused_computation.1 | loop fusion | flops 12582912 | bytes 16777216 | tf_op jit(solution)/shard_map/concatenate | solution.py:147
  123.7 12.0 %shard_map.73 = bf16[256,1024]{1,0:T(8,128)(2,1)} custom-call(s32[4]{0:T(128)} %or_select_fusion.slots_ref, s32[1]{0:T(128)S(6)} %copy.9.count_ref, bf16[256,1024]{1,0:T(8,128)(2,1)} %fusion.11.q_ref, bf16[2,8,256,1024]{3,2,1,0:T(8,128)(2,1)} %pad_maximum_fusion.refs_0_.refs_1_.refs_2_.refs_3_.refs_4_.refs_5_.refs_6_.refs_7_, ...), custom_call_target="tpu_custom_call" | custom-call | tf_op jit(solution)/shard_map/pallas_call | solution.py:51
  135.7 0.0 collective-permute-done.7
  135.7 1.4 %broadcast_select_fusion.1 = (bf16[1024,512]{1,0:T(8,128)(2,1)S(1)}, bf16[1024,512]{1,0:T(8,128)(2,1)S(1)}) fusion(bf16[1024,512]{1,0:T(8,128)(2,1)} %collective-permute-done.7, pred[]{:T(512)S(6)} %eq.21, bf16[32,32,512]{2,1,0:T(8,128)(2,1)S(1)} %all-to-all-done.1), kind=kLoop, calls=%fused_computation.21 | loop fusion | flops 1048576 | bytes 4194305 | tf_op jit(solution)/shard_map/jit(_where)/select_n | solution.py:119
  137.1 0.0 copy-done.1
  137.1 1.5 %fusion.14 = bf16[256,1024]{1,0:T(8,128)(2,1)} fusion(bf16[256,1024]{1,0:T(8,128)(2,1)S(1)} %copy-done.1, bf16[1024,512]{1,0:T(8,128)(2,1)S(1)} %get-tuple-element.10, bf16[1024,512]{1,0:T(8,128)(2,1)S(1)} %get-tuple-element.9), kind=kOutput, calls=%fused_computation.16 | convolution fusion | flops 541327360 | bytes 3145728 | tf_op jit(solution)/shard_map/dot_general | solution.py:150
  (9 shorter events, 0.1 us)
Async XLA Ops:
  0.0 1.9 %copy-start = (bf16[32,1024]{1,0:T(8,128)(2,1)S(1)}, bf16[32,1024]{1,0:T(8,128)(2,1)}, u32[]{:S(2)}) copy-start(bf16[32,1024]{1,0:T(8,128)(2,1)} %param.9) | copy-start | bytes 196612
  0.0 57.1 %copy-start.6 = (bf16[1024]{0:T(1024)(128)(2,1)S(1)}, bf16[1024]{0:T(1024)(128)(2,1)}, u32[]{:S(2)}) copy-start(bf16[1024]{0:T(1024)(128)(2,1)} %param.8) | copy-start | bytes 6148
  0.0 57.1 %copy-start.5 = (bf16[1024,32]{0,1:T(8,128)(2,1)S(1)}, bf16[1024,32]{0,1:T(8,128)(2,1)}, u32[]{:S(2)}) copy-start(bf16[1024,32]{0,1:T(8,128)(2,1)} %param.10) | copy-start | bytes 196612
  0.0 57.2 %copy-start.2 = (bf16[256,1024]{1,0:T(8,128)(2,1)S(1)}, bf16[256,1024]{1,0:T(8,128)(2,1)}, u32[]{:S(2)}) copy-start(bf16[256,1024]{1,0:T(8,128)(2,1)} %param.7) | copy-start | bytes 1572868
  1.2 0.8 collective-permute-start
  1.9 0.8 copy-start.3
  34.5 24.9 %collective-permute-start.1 = (bf16[1024,512]{1,0:T(8,128)(2,1)S(1)}, bf16[1024,512]{1,0:T(8,128)(2,1)S(1)}, u32[]{:S(2)}, u32[]{:S(2)}) collective-permute-start(bf16[1024,512]{1,0:T(8,128)(2,1)S(1)} %bitcast.22), channel_id=1, source_target_pairs={{0,32},{32,0},{64,96},{96,64},{128,160},{160,128},{192,224},{224,1... | collective-permute-start | bytes 3145736 | tf_op jit(solution)/shard_map/ppermute | solution.py:118
  61.1 12.9 %copy-start.4 = (bf16[2,2,64,1024]{3,2,1,0:T(8,128)(2,1)S(1)}, bf16[2,2,64,1024]{3,2,1,0:T(8,128)(2,1)}, u32[]{:S(2)}) copy-start(bf16[2,2,64,1024]{3,2,1,0:T(8,128)(2,1)} %copy-done.3) | copy-start | bytes 1572868
  61.2 15.0 %copy-start.7 = (s32[1,4]{1,0:T(1,128)S(1)}, s32[1,4]{1,0:T(1,128)}, u32[]{:S(2)}) copy-start(s32[1,4]{1,0:T(1,128)} %param.12) | copy-start | bytes 52
  62.2 37.4 %all-to-all-start.1 = ((bf16[32,32,512]{2,1,0:T(8,128)(2,1)}), bf16[32,32,512]{2,1,0:T(8,128)(2,1)S(1)}, u32[]{:S(2)}, u32[]{:S(2)}) async-start(bf16[32,32,512]{2,1,0:T(8,128)(2,1)} %tile.5), calls=%async_computation.1 | async-start | bytes 2097152 | tf_op jit(solution)/shard_map/all_to_all | solution.py:115
  67.8 49.2 %collective-permute-start.2 = (bf16[2,2,256,1024]{3,2,1,0:T(8,128)(2,1)}, bf16[2,2,256,1024]{3,2,1,0:T(8,128)(2,1)}, u32[]{:S(2)}, u32[]{:S(2)}) collective-permute-start(bf16[2,2,256,1024]{3,2,1,0:T(8,128)(2,1)} %param.11), channel_id=1, source_target_pairs={{0,32},{1,33},{2,34},{3,35},{4,36},{5,37},{6,38},{7,39},{8,40},{9,... | collective-permute-start | bytes 6291464 | tf_op jit(solution)/shard_map/ppermute | solution.py:68
  69.8 47.2 %collective-permute-start.3 = (bf16[2,2,256,1024]{3,2,1,0:T(8,128)(2,1)}, bf16[2,2,256,1024]{3,2,1,0:T(8,128)(2,1)}, u32[]{:S(2)}, u32[]{:S(2)}) collective-permute-start(bf16[2,2,256,1024]{3,2,1,0:T(8,128)(2,1)} %param.11), channel_id=1, source_target_pairs={{32,0},{33,1},{34,2},{35,3},{36,4},{37,5},{38,6},{39,7},{40,8},{41... | collective-permute-start | bytes 6291464 | tf_op jit(solution)/shard_map/ppermute | solution.py:69
  74.0 2.8 %collective-permute-start.4 = (bf16[2,2,64,1024]{3,2,1,0:T(8,128)(2,1)S(1)}, bf16[2,2,64,1024]{3,2,1,0:T(8,128)(2,1)S(1)}, u32[]{:S(2)}, u32[]{:S(2)}) collective-permute-start(bf16[2,2,64,1024]{3,2,1,0:T(8,128)(2,1)S(1)} %copy-done.4), channel_id=1, source_target_pairs={{224,252},{225,253},{226,254},{227,255},{228,224},{229,225},{230,2... | collective-permute-start | bytes 1572872 | tf_op jit(solution)/shard_map/ppermute | solution.py:94
  74.7 2.1 %collective-permute-start.5 = (bf16[2,2,64,1024]{3,2,1,0:T(8,128)(2,1)S(1)}, bf16[2,2,64,1024]{3,2,1,0:T(8,128)(2,1)S(1)}, u32[]{:S(2)}, u32[]{:S(2)}) collective-permute-start(bf16[2,2,64,1024]{3,2,1,0:T(8,128)(2,1)S(1)} %copy-done.4), channel_id=1, source_target_pairs={{224,232},{225,233},{226,234},{227,235},{228,236},{229,237},{230,2... | collective-permute-start | bytes 1572872 | tf_op jit(solution)/shard_map/ppermute | solution.py:94
  75.4 1.4 collective-permute-start.6
  99.6 36.1 %collective-permute-start.7 = (bf16[1024,512]{1,0:T(8,128)(2,1)S(1)}, bf16[1024,512]{1,0:T(8,128)(2,1)}, u32[]{:S(2)}, u32[]{:S(2)}) collective-permute-start(bf16[1024,512]{1,0:T(8,128)(2,1)S(1)} %bitcast.21), channel_id=1, source_target_pairs={{0,32},{32,0},{64,96},{96,64},{128,160},{160,128},{192,224},{224,1... | collective-permute-start | bytes 3145736 | tf_op jit(solution)/shard_map/ppermute | solution.py:118
  135.7 1.4 %copy-start.1 = (bf16[256,1024]{1,0:T(8,128)(2,1)S(1)}, bf16[256,1024]{1,0:T(8,128)(2,1)}, u32[]{:S(2)}) copy-start(bf16[256,1024]{1,0:T(8,128)(2,1)} %shard_map.73) | copy-start | bytes 1572868

commit v3 on v2

--- a/solution.py
+++ b/solution.py
@@ -9,8 +9,21 @@
 HD = 64
 
 
-def attention_kernel(slots_ref, count_ref, q_ref, *refs):
-    key_refs, value_refs, out_ref = refs[: (len(refs) - 1) // 2], refs[(len(refs) - 1) // 2 : -1], refs[-1]
+def attention_kernel(slots_ref, sources_ref, count_ref, q_ref, *refs):
+    nbr = slots_ref.shape[0]
+    per_part = len(refs[:-1]) // 2
+    sources = per_part // nbr
+    out_ref = refs[-1]
+
+    def block(part, slot):
+        first = part * per_part + slot * sources
+        picked = refs[first][...]
+        for source in range(1, sources):
+            picked = jnp.where(sources_ref[slot] == source, refs[first + source][...], picked)
+        return picked
+
+    keys = [block(0, slot) for slot in range(nbr)]
+    values = [block(1, slot) for slot in range(nbr)]
     count = count_ref[0]
     width = q_ref.shape[1]
     lane = lax.broadcasted_iota(jnp.int32, (1, width), 1)
@@ -20,40 +33,50 @@
         in_head = (lane >= head * HD) & (lane < (head + 1) * HD)
         q_head = jnp.where(in_head, q_all, jnp.zeros_like(q_all))
         scores = []
-        for slot, key_ref in enumerate(key_refs):
-            s = lax.dot_general(q_head, key_ref[...], (((1,), (1,)), ((), ())), preferred_element_type=jnp.float32)
+        for slot, key in enumerate(keys):
+            s = lax.dot_general(q_head, key, (((1,), (1,)), ((), ())), preferred_element_type=jnp.float32)
             scores.append(s if slot == 0 else jnp.where(slot < count, s, -jnp.inf))
         peak = scores[0].max(axis=1, keepdims=True)
         for s in scores[1:]:
             peak = jnp.maximum(peak, s.max(axis=1, keepdims=True))
         total = None
         mixed = None
-        for s, value_ref in zip(scores, value_refs):
+        for s, value in zip(scores, values):
             expo = jnp.exp(s - peak)
             part = expo.sum(axis=1, keepdims=True)
             total = part if total is None else total + part
-            term = jnp.dot(expo.astype(jnp.bfloat16), value_ref[...], preferred_element_type=jnp.float32)
+            term = jnp.dot(expo.astype(jnp.bfloat16), value, preferred_element_type=jnp.float32)
             mixed = term if mixed is None else mixed + term
         head_out = mixed / total
         result = head_out if result is None else jnp.where(in_head, head_out, result)
     out_ref[...] = result.astype(out_ref.dtype)
 
 
-def attend(q, window, slots, count, lanes=128):
+def attend(q, banks, slots, sources, count, lanes=128):
     rows, width = q.shape
     nbr = slots.shape[0]
-    q_spec = pl.BlockSpec((rows, lanes), lambda h, s, c: (0, h))
+    q_spec = pl.BlockSpec((rows, lanes), lambda h, s, src, c: (0, h))
 
-    def kv_spec(part, slot):
-        return pl.BlockSpec((None, None, rows, lanes), lambda h, s, c: (part, s[slot], 0, h))
+    def kv_spec(part, slot, source):
+        def index(h, s, src, c):
+            used = src[slot] == source
+            return (part, jnp.where(used, s[slot], 0), 0, jnp.where(used, h, 0))
 
-    in_specs = [q_spec] + [kv_spec(0, j) for j in range(nbr)] + [kv_spec(1, j) for j in range(nbr)]
+        return pl.BlockSpec((None, None, rows, lanes), index)
+
+    in_specs = [q_spec]
+    operands = []
+    for part in range(2):
+        for slot in range(nbr):
+            for source, bank in enumerate(banks):
+                in_specs.append(kv_spec(part, slot, source))
+                operands.append(bank)
     return pl.pallas_call(
         attention_kernel,
         grid_spec=pltpu.PrefetchScalarGridSpec(
-            num_scalar_prefetch=2, grid=(width // lanes,), in_specs=in_specs, out_specs=q_spec),
+            num_scalar_prefetch=3, grid=(width // lanes,), in_specs=in_specs, out_specs=q_spec),
         out_shape=jax.ShapeDtypeStruct((rows, width), jnp.bfloat16),
-    )(slots, count, q, *([window] * (2 * nbr)))
+    )(slots, sources, count, q, *operands)
 
 
 Y_LO = 4
@@ -140,12 +163,12 @@
     crossing = ((lat == split) & (local_lists < blocks_here)) | (
         (lat == split - 1) & (local_lists >= 2 * blocks_here)
     )
-    slots = jnp.where(crossing, 3 * blocks_here + local_lists % blocks_here, local_lists)
+    slots = local_lists % blocks_here
+    sources = jnp.where(crossing, 3, local_lists // blocks_here)
     moved = far_side(sent[2])
     below, above, own = sent
     joined = assembled(kv_cache, own, moved)
-    window = jnp.concatenate([below, kv_cache, above, joined], axis=1)
-    attended = attend(query, window, slots, counts)
+    attended = attend(query, (below, kv_cache, above, joined), slots, sources, counts)
     w_out_rows = gathered_rows(w_out.T, after=query)
     decoded = lax.dot_general(
         attended,
@@ -166,4 +189,6 @@
         P(("lat", "lon"), None),
         P(("lat", "lon")),
     )
-    return jax.shard_map(layer, mesh=mesh, in_specs=placed, out_specs=P(("lat", "lon"), None), check_vma=False)
+    return jax.shard_map(
+        layer, mesh=mesh, in_specs=placed, out_specs=P(("lat", "lon"), None), check_vma=False
+    )

time: 140 us -> 142 us (1.014)
  the two profiles are of different devices: /device:TPU:6 before, /device:TPU:7 now
where the time goes in v3:
time: 142 us; the launch traced here: 141 us
  waiting for transfers between devices  39.5 us (28%)
  blocking collectives  33.9 us (24%)
  starting transfers between devices  31 us (22%)
  Pallas kernels  16.9 us (12%)
  local copies, waits for them, and re-layouts  8.36 us (6%)
  other arithmetic  7.45 us (5%)
  matrix products  3.1 us (2%)
    all_to_all x1, blocking collectives, gathered_rows(): lax.all_to_all(jnp.tile(mine, (lon_count, 1)), 'lon', 0, 0, tiled=True)  33.9 us
    ppermute x3, waiting for transfers between devices, along_z(): return lax.ppermute(value, both, pairs)  23.3 us
    pallas_call x1, Pallas kernels, attend(): pl.pallas_call(attention_kernel, grid_spec=pltpu.PrefetchScalarGridSpec(n...  16.9 us
    ppermute x1, waiting for transfers between devices, neighbour_bands(): own = lax.ppermute(piece, both, cross)  13.8 us
    ppermute x3, starting transfers between devices, along_z(): return lax.ppermute(value, both, pairs)  9.52 us
    ppermute x1, starting transfers between devices, neighbour_bands(): own = lax.ppermute(piece, both, cross)  5.57 us
    all_to_all x1, starting transfers between devices, gathered_rows(): lax.all_to_all(jnp.tile(mine, (lon_count, 1)), 'lon', 0, 0, tiled=True)  5.23 us
    ppermute x2, starting transfers between devices, gathered_rows(): other = lax.ppermute(fetched, 'lat', swap)  5.06 us
  transfers between devices with their start and end apart: 9, of which 5 were waited for; matrix products, arithmetic and copies ran while one was open for 8% of the time, Pallas kernels for 12%

profile of v3, /device:TPU:7, one launch (start us, length us, event | category | flops | bytes accessed | tf_op | source)
XLA Modules:
  0.0 141.1 jit_solution(4604520399746020461)
XLA Ops:
  0.0 0.0 copy-start
  0.0 0.0 copy-start.6
  0.0 0.0 copy-start.5
  0.0 0.0 copy-start.3
  0.0 1.1 constant_dynamic-slice_fusion
  1.2 5.6 %collective-permute-start = (bf16[2,2,64,1024]{3,2,1,0:T(8,128)(2,1)S(1)}, bf16[2,2,64,1024]{3,2,1,0:T(8,128)(2,1)S(1)}, u32[]{:S(2)}, u32[]{:S(2)}) collective-permute-start(bf16[2,2,64,1024]{3,2,1,0:T(8,128)(2,1)S(1)} %constant_dynamic-slice_fusion), channel_id=1, source_target_pairs={{224,259},{256,227},{225,258},{257,226},{226,257},{258,225},{227,2... | collective-permute-start | bytes 1572872 | tf_op jit(solution)/shard_map/ppermute | solution.py:101
  6.8 0.0 copy-done
  6.8 13.8 %collective-permute-done = bf16[2,2,64,1024]{3,2,1,0:T(8,128)(2,1)S(1)} collective-permute-done((bf16[2,2,64,1024]{3,2,1,0:T(8,128)(2,1)S(1)}, bf16[2,2,64,1024]{3,2,1,0:T(8,128)(2,1)S(1)}, u32[]{:S(2)}, u32[]{:S(2)}) %collective-permute-start) | collective-permute-done | bytes 524320 | tf_op jit(solution)/shard_map/ppermute | solution.py:101
  20.6 0.0 copy-start.4
  20.6 0.8 copy-done.4
  21.4 0.1 tile.4
  21.5 33.9 %all_to_all.18 = bf16[32,32,512]{2,1,0:T(8,128)(2,1)S(1)} all-to-all(bf16[32,32,512]{2,1,0:T(8,128)(2,1)S(1)} %tile.4), channel_id=1, replica_groups=mesh['lat'=16,'lon'=32] {'lon'}, dimensions={0} | all-to-all | bytes 2097152 | tf_op jit(solution)/shard_map/all_to_all | solution.py:138
  55.4 1.9 %collective-permute-start.1 = (bf16[1024,512]{1,0:T(8,128)(2,1)S(1)}, bf16[1024,512]{1,0:T(8,128)(2,1)S(1)}, u32[]{:S(2)}, u32[]{:S(2)}) collective-permute-start(bf16[1024,512]{1,0:T(8,128)(2,1)S(1)} %bitcast.42), channel_id=1, source_target_pairs={{0,32},{32,0},{64,96},{96,64},{128,160},{160,128},{192,224},{224,1... | collective-permute-start | bytes 3145736 | tf_op jit(solution)/shard_map/ppermute | solution.py:141
  57.3 0.0 copy-done.6
  57.3 0.0 copy-done.5
  57.4 0.0 copy-done.3
  57.4 0.2 fusion.17
  57.6 2.4 %collective-permute-done.1 = bf16[1024,512]{1,0:T(8,128)(2,1)S(1)} collective-permute-done((bf16[1024,512]{1,0:T(8,128)(2,1)S(1)}, bf16[1024,512]{1,0:T(8,128)(2,1)S(1)}, u32[]{:S(2)}, u32[]{:S(2)}) %collective-permute-start.1) | collective-permute-done | bytes 1048608 | tf_op jit(solution)/shard_map/ppermute | solution.py:141
  59.9 0.2 broadcast_select_fusion.3
  60.1 1.6 %fusion.11.q_ref = bf16[256,1024]{1,0:T(8,128)(2,1)} fusion(bf16[1024,512]{1,0:T(8,128)(2,1)S(1)} %get-tuple-element.12, bf16[1024,512]{1,0:T(8,128)(2,1)S(1)} %get-tuple-element.11, bf16[256,1024]{1,0:T(8,128)(2,1)S(1)} %copy-done.3, f32[1024]{0:T(1024)S(1)} %convert_element_type.16, f32[256]{0:T(256)S(1)} %add_rsqrt_fusion), kind=kOutput, calls=%fused_computation.14 | convolution fusion | flops 542638080 | bytes 3150848 | tf_op jit(solution)/shard_map/dot_general | solution.py:154
  61.7 0.0 copy-start.1
  61.7 1.1 tile.5
  62.8 5.2 %all-to-all-start.1 = ((bf16[32,32,512]{2,1,0:T(8,128)(2,1)}), bf16[32,32,512]{2,1,0:T(8,128)(2,1)S(1)}, u32[]{:S(2)}, u32[]{:S(2)}) async-start(bf16[32,32,512]{2,1,0:T(8,128)(2,1)} %tile.5), calls=%async_computation.1 | async-start | bytes 2097152 | tf_op jit(solution)/shard_map/all_to_all | solution.py:138
  68.0 0.0 copy-done.1
  68.1 1.3 collective-permute-start.2
  69.4 4.4 %collective-permute-start.3 = (bf16[2,2,256,1024]{3,2,1,0:T(8,128)(2,1)S(1)}, bf16[2,2,256,1024]{3,2,1,0:T(8,128)(2,1)}, u32[]{:S(2)}, u32[]{:S(2)}) collective-permute-start(bf16[2,2,256,1024]{3,2,1,0:T(8,128)(2,1)S(1)} %copy-done.1), channel_id=1, source_target_pairs={{32,0},{33,1},{34,2},{35,3},{36,4},{37,5},{38,6},{39,7},{40,8},{41... | collective-permute-start | bytes 6291464 | tf_op jit(solution)/shard_map/ppermute | solution.py:92
  73.7 4.6 %collective-permute-start.4 = (bf16[2,2,64,1024]{3,2,1,0:T(8,128)(2,1)}, bf16[2,2,64,1024]{3,2,1,0:T(8,128)(2,1)}, u32[]{:S(2)}, u32[]{:S(2)}) collective-permute-start(bf16[2,2,64,1024]{3,2,1,0:T(8,128)(2,1)} %copy-done.4), channel_id=1, source_target_pairs={{224,252},{225,253},{226,254},{227,255},{228,224},{229,225},{230,2... | collective-permute-start | bytes 1572872 | tf_op jit(solution)/shard_map/ppermute | solution.py:117
  79.0 1.9 %collective-permute-start.5 = (bf16[2,2,64,1024]{3,2,1,0:T(8,128)(2,1)}, bf16[2,2,64,1024]{3,2,1,0:T(8,128)(2,1)}, u32[]{:S(2)}, u32[]{:S(2)}) collective-permute-start(bf16[2,2,64,1024]{3,2,1,0:T(8,128)(2,1)} %copy-done.4), channel_id=1, source_target_pairs={{224,232},{225,233},{226,234},{227,235},{228,236},{229,237},{230,2... | collective-permute-start | bytes 1572872 | tf_op jit(solution)/shard_map/ppermute | solution.py:117
  80.9 3.0 %collective-permute-start.6 = (bf16[2,2,64,1024]{3,2,1,0:T(8,128)(2,1)}, bf16[2,2,64,1024]{3,2,1,0:T(8,128)(2,1)}, u32[]{:S(2)}, u32[]{:S(2)}) collective-permute-start(bf16[2,2,64,1024]{3,2,1,0:T(8,128)(2,1)} %copy-done.4), channel_id=1, source_target_pairs={{224,228},{225,229},{226,230},{227,231},{228,232},{229,233},{230,2... | collective-permute-start | bytes 1572872 | tf_op jit(solution)/shard_map/ppermute | solution.py:117
  83.9 15.3 %collective-permute-done.4 = bf16[2,2,64,1024]{3,2,1,0:T(8,128)(2,1)} collective-permute-done((bf16[2,2,64,1024]{3,2,1,0:T(8,128)(2,1)}, bf16[2,2,64,1024]{3,2,1,0:T(8,128)(2,1)}, u32[]{:S(2)}, u32[]{:S(2)}) %collective-permute-start.4) | collective-permute-done | bytes 524320 | tf_op jit(solution)/shard_map/ppermute | solution.py:117
  99.2 0.0 all-to-all-done.1
  99.2 3.1 %collective-permute-start.7 = (bf16[1024,512]{1,0:T(8,128)(2,1)S(1)}, bf16[1024,512]{1,0:T(8,128)(2,1)}, u32[]{:S(2)}, u32[]{:S(2)}) collective-permute-start(bf16[1024,512]{1,0:T(8,128)(2,1)S(1)} %bitcast.41), channel_id=1, source_target_pairs={{0,32},{32,0},{64,96},{96,64},{128,160},{160,128},{192,224},{224,1... | collective-permute-start | bytes 3145736 | tf_op jit(solution)/shard_map/ppermute | solution.py:141
  102.4 0.0 copy-done.7
  102.4 0.6 or_select_fusion
  103.0 3.8 %collective-permute-done.5 = bf16[2,2,64,1024]{3,2,1,0:T(8,128)(2,1)} collective-permute-done((bf16[2,2,64,1024]{3,2,1,0:T(8,128)(2,1)}, bf16[2,2,64,1024]{3,2,1,0:T(8,128)(2,1)}, u32[]{:S(2)}, u32[]{:S(2)}) %collective-permute-start.5) | collective-permute-done | bytes 524320 | tf_op jit(solution)/shard_map/ppermute | solution.py:117
  106.8 4.2 %collective-permute-done.6 = bf16[2,2,64,1024]{3,2,1,0:T(8,128)(2,1)} collective-permute-done((bf16[2,2,64,1024]{3,2,1,0:T(8,128)(2,1)}, bf16[2,2,64,1024]{3,2,1,0:T(8,128)(2,1)}, u32[]{:S(2)}, u32[]{:S(2)}) %collective-permute-start.6) | collective-permute-done | bytes 524320 | tf_op jit(solution)/shard_map/ppermute | solution.py:117
  111.0 3.1 %pad_maximum_fusion = bf16[4,2,2,64,1024]{4,3,2,1,0:T(8,128)(2,1)} fusion(bf16[1,2,2,64,1024]{4,3,2,1,0:T(8,128)(2,1)} %bitcast.5, bf16[1,2,2,64,1024]{4,3,2,1,0:T(8,128)(2,1)} %bitcast.4, bf16[1,2,2,64,1024]{4,3,2,1,0:T(8,128)(2,1)} %bitcast.3, bf16[1,2,2,64,1024]{4,3,2,1,0:T(8,128)(2,1)} %bitcast.43), kind=kLoop, calls=%fused_computation.5 | loop fusion | flops 3145728 | bytes 4194304 | tf_op jit(solution)/shard_map/stack | solution.py:125
  114.2 3.6 %gather_fusion = bf16[4,2,2,64,1024]{4,3,2,1,0:T(8,128)(2,1)} fusion(bf16[4,2,2,64,1024]{4,3,2,1,0:T(8,128)(2,1)} %pad_maximum_fusion, s32[1024]{0:T(1024)S(1)} %pad_clamp_fusion), kind=kCustom, calls=%fused_computation | custom fusion | bytes 4194320 | tf_op jit(solution)/shard_map/jit(_take)/gather | solution.py:127
  117.8 1.9 %select_bitcast_fusion = bf16[2,2,4,64,1024]{4,3,1,0,2:T(8,128)(2,1)S(1)} fusion(bf16[4,2,2,64,1024]{4,3,2,1,0:T(8,128)(2,1)} %gather_fusion, pred[4]{0:T(512)(128)(4,1)S(1)} %compare_and_fusion), kind=kLoop, calls=%fused_computation.10 | loop fusion | flops 1048576 | bytes 4194308 | tf_op jit(solution)/shard_map/jit(_take)/select_n | solution.py:127
  119.7 1.5 %copy.8 = bf16[2,2,4,64,1024]{4,3,2,1,0:T(8,128)(2,1)} copy(bf16[2,2,4,64,1024]{4,3,1,0,2:T(8,128)(2,1)S(1)} %select_bitcast_fusion) | data formatting | bytes 4194304 | tf_op jit(solution)/shard_map/jit(_take)/select_n | solution.py:127
  121.2 0.0 collective-permute-done.2.refs_0_.refs_4_.refs_8_.refs_12_.refs_16_.refs_20_.refs_24_.refs_28_
  121.2 0.0 collective-permute-done.3.refs_2_.refs_6_.refs_10_.refs_14_.refs_18_.refs_22_.refs_26_.refs_30_
  121.2 16.9 %shard_map.73 = bf16[256,1024]{1,0:T(8,128)(2,1)} custom-call(s32[4]{0:T(128)} %get-tuple-element.14.slots_ref, s32[4]{0:T(128)} %get-tuple-element.13.sources_ref, s32[1]{0:T(128)S(6)} %copy.9.count_ref, bf16[256,1024]{1,0:T(8,128)(2,1)} %fusion.11.q_ref, ...), custom_call_target="tpu_custom_call" | custom-call | tf_op jit(solution)/shard_map/pallas_call | solution.py:74
  138.1 0.0 copy-start.2
  138.1 0.0 collective-permute-done.7
  138.2 1.4 %broadcast_select_fusion.1 = (bf16[1024,512]{1,0:T(8,128)(2,1)S(1)}, bf16[1024,512]{1,0:T(8,128)(2,1)S(1)}) fusion(bf16[1024,512]{1,0:T(8,128)(2,1)} %collective-permute-done.7, pred[]{:T(512)S(6)} %eq.21, bf16[32,32,512]{2,1,0:T(8,128)(2,1)S(1)} %all-to-all-done.1), kind=kLoop, calls=%fused_computation.20 | loop fusion | flops 1048576 | bytes 4194305 | tf_op jit(solution)/shard_map/jit(_where)/select_n | solution.py:142
  139.6 0.0 copy-done.2
  139.6 1.5 %fusion.14 = bf16[256,1024]{1,0:T(8,128)(2,1)} fusion(bf16[256,1024]{1,0:T(8,128)(2,1)S(1)} %copy-done.2, bf16[1024,512]{1,0:T(8,128)(2,1)S(1)} %get-tuple-element.10, bf16[1024,512]{1,0:T(8,128)(2,1)S(1)} %get-tuple-element.9), kind=kOutput, calls=%fused_computation.15 | convolution fusion | flops 541327360 | bytes 3145728 | tf_op jit(solution)/shard_map/dot_general | solution.py:173
  (8 shorter events, 0.1 us)
Async XLA Ops:
  0.0 6.8 %copy-start = (bf16[32,1024]{1,0:T(8,128)(2,1)S(1)}, bf16[32,1024]{1,0:T(8,128)(2,1)}, u32[]{:S(2)}) copy-start(bf16[32,1024]{1,0:T(8,128)(2,1)} %param.9) | copy-start | bytes 196612
  0.0 57.3 %copy-start.6 = (bf16[1024]{0:T(1024)(128)(2,1)S(1)}, bf16[1024]{0:T(1024)(128)(2,1)}, u32[]{:S(2)}) copy-start(bf16[1024]{0:T(1024)(128)(2,1)} %param.8) | copy-start | bytes 6148
  0.0 57.3 %copy-start.5 = (bf16[1024,32]{0,1:T(8,128)(2,1)S(1)}, bf16[1024,32]{0,1:T(8,128)(2,1)}, u32[]{:S(2)}) copy-start(bf16[1024,32]{0,1:T(8,128)(2,1)} %param.10) | copy-start | bytes 196612
  0.0 57.4 %copy-start.3 = (bf16[256,1024]{1,0:T(8,128)(2,1)S(1)}, bf16[256,1024]{1,0:T(8,128)(2,1)}, u32[]{:S(2)}) copy-start(bf16[256,1024]{1,0:T(8,128)(2,1)} %param.7) | copy-start | bytes 1572868
  1.2 19.4 %collective-permute-start = (bf16[2,2,64,1024]{3,2,1,0:T(8,128)(2,1)S(1)}, bf16[2,2,64,1024]{3,2,1,0:T(8,128)(2,1)S(1)}, u32[]{:S(2)}, u32[]{:S(2)}) collective-permute-start(bf16[2,2,64,1024]{3,2,1,0:T(8,128)(2,1)S(1)} %constant_dynamic-slice_fusion), channel_id=1, source_target_pairs={{224,259},{256,227},{225,258},{257,226},{226,257},{258,225},{227,2... | collective-permute-start | bytes 1572872 | tf_op jit(solution)/shard_map/ppermute | solution.py:101
  20.6 0.8 copy-start.4
  55.4 4.5 %collective-permute-start.1 = (bf16[1024,512]{1,0:T(8,128)(2,1)S(1)}, bf16[1024,512]{1,0:T(8,128)(2,1)S(1)}, u32[]{:S(2)}, u32[]{:S(2)}) collective-permute-start(bf16[1024,512]{1,0:T(8,128)(2,1)S(1)} %bitcast.42), channel_id=1, source_target_pairs={{0,32},{32,0},{64,96},{96,64},{128,160},{160,128},{192,224},{224,1... | collective-permute-start | bytes 3145736 | tf_op jit(solution)/shard_map/ppermute | solution.py:141
  61.7 6.3 %copy-start.1 = (bf16[2,2,256,1024]{3,2,1,0:T(8,128)(2,1)S(1)}, bf16[2,2,256,1024]{3,2,1,0:T(8,128)(2,1)}, u32[]{:S(2)}) copy-start(bf16[2,2,256,1024]{3,2,1,0:T(8,128)(2,1)} %refs_29_.1) | copy-start | bytes 6291460
  61.7 40.7 %copy-start.7 = (s32[1,4]{1,0:T(1,128)S(1)}, s32[1,4]{1,0:T(1,128)}, u32[]{:S(2)}) copy-start(s32[1,4]{1,0:T(1,128)} %param.12) | copy-start | bytes 52
  62.8 36.4 %all-to-all-start.1 = ((bf16[32,32,512]{2,1,0:T(8,128)(2,1)}), bf16[32,32,512]{2,1,0:T(8,128)(2,1)S(1)}, u32[]{:S(2)}, u32[]{:S(2)}) async-start(bf16[32,32,512]{2,1,0:T(8,128)(2,1)} %tile.5), calls=%async_computation.1 | async-start | bytes 2097152 | tf_op jit(solution)/shard_map/all_to_all | solution.py:138
  68.1 53.1 %collective-permute-start.2 = (bf16[2,2,256,1024]{3,2,1,0:T(8,128)(2,1)S(1)}, bf16[2,2,256,1024]{3,2,1,0:T(8,128)(2,1)}, u32[]{:S(2)}, u32[]{:S(2)}) collective-permute-start(bf16[2,2,256,1024]{3,2,1,0:T(8,128)(2,1)S(1)} %copy-done.1), channel_id=1, source_target_pairs={{0,32},{1,33},{2,34},{3,35},{4,36},{5,37},{6,38},{7,39},{8,40},{9,... | collective-permute-start | bytes 6291464 | tf_op jit(solution)/shard_map/ppermute | solution.py:91
  69.4 51.8 %collective-permute-start.3 = (bf16[2,2,256,1024]{3,2,1,0:T(8,128)(2,1)S(1)}, bf16[2,2,256,1024]{3,2,1,0:T(8,128)(2,1)}, u32[]{:S(2)}, u32[]{:S(2)}) collective-permute-start(bf16[2,2,256,1024]{3,2,1,0:T(8,128)(2,1)S(1)} %copy-done.1), channel_id=1, source_target_pairs={{32,0},{33,1},{34,2},{35,3},{36,4},{37,5},{38,6},{39,7},{40,8},{41... | collective-permute-start | bytes 6291464 | tf_op jit(solution)/shard_map/ppermute | solution.py:92
  73.7 25.5 %collective-permute-start.4 = (bf16[2,2,64,1024]{3,2,1,0:T(8,128)(2,1)}, bf16[2,2,64,1024]{3,2,1,0:T(8,128)(2,1)}, u32[]{:S(2)}, u32[]{:S(2)}) collective-permute-start(bf16[2,2,64,1024]{3,2,1,0:T(8,128)(2,1)} %copy-done.4), channel_id=1, source_target_pairs={{224,252},{225,253},{226,254},{227,255},{228,224},{229,225},{230,2... | collective-permute-start | bytes 1572872 | tf_op jit(solution)/shard_map/ppermute | solution.py:117
  79.0 27.8 %collective-permute-start.5 = (bf16[2,2,64,1024]{3,2,1,0:T(8,128)(2,1)}, bf16[2,2,64,1024]{3,2,1,0:T(8,128)(2,1)}, u32[]{:S(2)}, u32[]{:S(2)}) collective-permute-start(bf16[2,2,64,1024]{3,2,1,0:T(8,128)(2,1)} %copy-done.4), channel_id=1, source_target_pairs={{224,232},{225,233},{226,234},{227,235},{228,236},{229,237},{230,2... | collective-permute-start | bytes 1572872 | tf_op jit(solution)/shard_map/ppermute | solution.py:117
  80.9 30.1 %collective-permute-start.6 = (bf16[2,2,64,1024]{3,2,1,0:T(8,128)(2,1)}, bf16[2,2,64,1024]{3,2,1,0:T(8,128)(2,1)}, u32[]{:S(2)}, u32[]{:S(2)}) collective-permute-start(bf16[2,2,64,1024]{3,2,1,0:T(8,128)(2,1)} %copy-done.4), channel_id=1, source_target_pairs={{224,228},{225,229},{226,230},{227,231},{228,232},{229,233},{230,2... | collective-permute-start | bytes 1572872 | tf_op jit(solution)/shard_map/ppermute | solution.py:117
  99.2 39.0 %collective-permute-start.7 = (bf16[1024,512]{1,0:T(8,128)(2,1)S(1)}, bf16[1024,512]{1,0:T(8,128)(2,1)}, u32[]{:S(2)}, u32[]{:S(2)}) collective-permute-start(bf16[1024,512]{1,0:T(8,128)(2,1)S(1)} %bitcast.41), channel_id=1, source_target_pairs={{0,32},{32,0},{64,96},{96,64},{128,160},{160,128},{192,224},{224,1... | collective-permute-start | bytes 3145736 | tf_op jit(solution)/shard_map/ppermute | solution.py:141
  138.1 1.4 %copy-start.2 = (bf16[256,1024]{1,0:T(8,128)(2,1)S(1)}, bf16[256,1024]{1,0:T(8,128)(2,1)}, u32[]{:S(2)}) copy-start(bf16[256,1024]{1,0:T(8,128)(2,1)} %shard_map.73) | copy-start | bytes 1572868

commit v4 on v1

--- a/solution.py
+++ b/solution.py
@@ -79,13 +79,10 @@
     return below, above, own
 
 
-def far_side(kv, below, above, own):
+def far_side(own):
     lat_count, lon_count = lax.axis_size("lat"), lax.axis_size("lon")
-    lat, lon = lax.axis_index("lat"), lax.axis_index("lon")
     both = ("lat", "lon")
     split = lat_count // 2
-    rows = kv.shape[2] // Y_LO
-    z = lon // Y_LO
     z_count = lon_count // Y_LO
 
     def along_z(value, shift):
@@ -96,11 +93,16 @@
                 pairs.append((band * lon_count + l, band * lon_count + target))
         return lax.ppermute(value, both, pairs)
 
-    half = rows // 2
-    opposite = jnp.concatenate(
-        [along_z(own[:, :, :half], 2), along_z(own[:, :, half:], -2)], axis=2
-    )
-    quarters = jnp.stack([own, along_z(own, -1), opposite, along_z(own, 1)])
+    moved = [along_z(own, 2), along_z(own, -1), along_z(own, 1)]
+    return moved
+
+
+def assembled(kv, below, above, own, moved):
+    lat_count = lax.axis_size("lat")
+    lat, lon = lax.axis_index("lat"), lax.axis_index("lon")
+    split = lat_count // 2
+    z = lon // Y_LO
+    quarters = jnp.stack([own, moved[1], moved[0], moved[2]])
     order = (jnp.arange(Y_LO) - z) % Y_LO
     joined = jnp.take(quarters, order, axis=0)
     joined = jnp.moveaxis(joined, 0, 2).reshape(kv.shape)
@@ -120,9 +122,7 @@
     lat_count = lax.axis_size("lat")
     swap = [(i, i ^ 1) for i in range(lat_count)]
     other = lax.ppermute(fetched, "lat", swap)
-    low = jnp.where(core == 0, fetched, other)
-    high = jnp.where(core == 0, other, fetched)
-    return jnp.concatenate([low, high], axis=1)
+    return fetched, other
 
 
 def layer(queries, gain, w_query, w_out, kv_cache, nbr_lists, counts):
@@ -132,24 +132,25 @@
     blocks_here = kv_cache.shape[1]
     sent = neighbour_bands(kv_cache)
     w_query_rows = gathered_rows(w_query, after=sent[2])
-    projected = jnp.dot(
-        normed,
-        w_query_rows,
-        preferred_element_type=jnp.float32,
+    core = lax.axis_index("lat") % 2
+    mine, theirs = (
+        (jnp.dot(normed, half, preferred_element_type=jnp.float32) * HD ** (-0.5)).astype(jnp.bfloat16)
+        for half in w_query_rows
     )
-    query = (projected * HD ** (-0.5)).astype(jnp.bfloat16)
+    query = jnp.where(core == 0, jnp.concatenate([mine, theirs], axis=1), jnp.concatenate([theirs, mine], axis=1))
     local_lists = nbr_lists - (lax.axis_index("lat") - 1) * blocks_here
     slots = jnp.clip(local_lists[0], 0, 3 * blocks_here - 1)
-    below, above = far_side(kv_cache, *sent)
+    moved = far_side(sent[2])
+    below, above = assembled(kv_cache, *sent, moved)
     window = jnp.concatenate([below, kv_cache, above], axis=1)
     attended = attend(query, window, slots, counts)
     w_out_rows = gathered_rows(w_out.T, after=query)
-    decoded = lax.dot_general(
-        attended,
-        w_out_rows,
-        (((1,), (1,)), ((), ())),
-        preferred_element_type=jnp.float32,
-    )
+    half = attended.shape[1] // 2
+    own_half = lax.dynamic_slice_in_dim(attended, core * half, half, axis=1)
+    other_half = lax.dynamic_slice_in_dim(attended, (1 - core) * half, half, axis=1)
+    contract = (((1,), (1,)), ((), ()))
+    decoded = lax.dot_general(own_half, w_out_rows[0], contract, preferred_element_type=jnp.float32)
+    decoded = decoded + lax.dot_general(other_half, w_out_rows[1], contract, preferred_element_type=jnp.float32)
     return decoded.astype(jnp.bfloat16)
 
 

time: 143 us -> 142 us (level)
  starting transfers between devices: 62 us -> 59.3 us
  waiting for transfers between devices: 16.3 us -> 18.3 us
  other arithmetic: 12.4 us -> 10.7 us
    all_to_all x1, waiting for transfers between devices: 14.3 us -> 16.8 us  [gathered_rows(): lax.all_to_all(jnp.tile(mine, (lon_count, 1)), 'lon', 0, 0, tiled=True)]
    ppermute x4 -> x3, starting transfers between devices: 3.44 us -> 2.08 us  [along_z(): return lax.ppermute(value, both, pairs)]
    dot_general x2 -> x4, matrix products: 3.09 us -> 4.07 us  [the longest x1 1.83 us: layer(): lax.dot_general(other_half, w_out_rows[1], contract, preferred_element_ty...]
    select_n x5 -> x4, other arithmetic: 4.51 us -> 3.82 us  [the longest x1 2.61 us: assembled(): below = jnp.where(lat == split, joined, below)]
  transfers between devices with their start and end apart: 10 -> 9, of which waited for: 2 -> 2; matrix products, arithmetic and copies ran while one was open for 9% -> 9% of each run, Pallas kernels for 8% -> 9%
where the time goes in v4:
time: 142 us; the launch traced here: 140 us
  starting transfers between devices  59.3 us (42%)
  blocking collectives  30 us (21%)
  waiting for transfers between devices  18.3 us (13%)
  Pallas kernels  12 us (8%)
  other arithmetic  10.7 us (8%)
  local copies, waits for them, and re-layouts  4.96 us (3%)
  matrix products  4.07 us (3%)
    ppermute x2, starting transfers between devices, gathered_rows(): other = lax.ppermute(fetched, 'lat', swap)  45.8 us
    all_to_all x1, blocking collectives, gathered_rows(): lax.all_to_all(jnp.tile(mine, (lon_count, 1)), 'lon', 0, 0, tiled=True)  30 us
    all_to_all x1, waiting for transfers between devices, gathered_rows(): lax.all_to_all(jnp.tile(mine, (lon_count, 1)), 'lon', 0, 0, tiled=True)  16.8 us
    pallas_call x1, Pallas kernels, attend(): pl.pallas_call(attention_kernel, grid_spec=pltpu.PrefetchScalarGridSpec(n...  12 us
    all_to_all x1, starting transfers between devices, gathered_rows(): lax.all_to_all(jnp.tile(mine, (lon_count, 1)), 'lon', 0, 0, tiled=True)  5.11 us
    concatenate x1, other arithmetic, layer(): window = jnp.concatenate([below, kv_cache, above], axis=1)  4.53 us
    ppermute x1, starting transfers between devices, neighbour_bands(): above = lax.ppermute(kv, both, [(j, i) for i, j in up])  3.73 us
  transfers between devices with their start and end apart: 9, of which 2 were waited for; matrix products, arithmetic and copies ran while one was open for 9% of the time, Pallas kernels for 9%

profile of v4, /device:TPU:57, one launch (start us, length us, event | category | flops | bytes accessed | tf_op | source)
XLA Modules:
  0.0 140.4 jit_solution(17313169952549054646)
XLA Ops:
  0.0 0.0 copy-start
  0.0 0.0 copy-start.4
  0.0 0.0 copy-start.3
  0.0 0.0 copy-start.2
  0.0 1.1 constant_dynamic-slice_fusion
  1.2 0.7 collective-permute-start
  1.9 0.0 copy-done
  1.9 0.0 collective-permute-done
  1.9 0.1 tile.4
  2.0 30.0 %all_to_all.18 = bf16[32,32,512]{2,1,0:T(8,128)(2,1)S(1)} all-to-all(bf16[32,32,512]{2,1,0:T(8,128)(2,1)S(1)} %tile.4), channel_id=1, replica_groups=mesh['lat'=16,'lon'=32] {'lon'}, dimensions={0} | all-to-all | bytes 2097152 | tf_op jit(solution)/shard_map/all_to_all | solution.py:121
  32.1 26.2 %collective-permute-start.1 = (bf16[1024,512]{1,0:T(8,128)(2,1)S(1)}, bf16[1024,512]{1,0:T(8,128)(2,1)S(1)}, u32[]{:S(2)}, u32[]{:S(2)}) collective-permute-start(bf16[1024,512]{1,0:T(8,128)(2,1)S(1)} %bitcast.23), channel_id=1, source_target_pairs={{0,32},{32,0},{64,96},{96,64},{128,160},{160,128},{192,224},{224,1... | collective-permute-start | bytes 3145736 | tf_op jit(solution)/shard_map/ppermute | solution.py:124
  58.3 0.0 copy-done.4
  58.3 0.0 copy-done.3
  58.3 0.0 copy-done.2
  58.3 0.2 fusion.2
  58.5 0.5 fusion
  59.0 1.5 %collective-permute-done.1 = bf16[1024,512]{1,0:T(8,128)(2,1)S(1)} collective-permute-done((bf16[1024,512]{1,0:T(8,128)(2,1)S(1)}, bf16[1024,512]{1,0:T(8,128)(2,1)S(1)}, u32[]{:S(2)}, u32[]{:S(2)}) %collective-permute-start.1) | collective-permute-done | bytes 1048608 | tf_op jit(solution)/shard_map/ppermute | solution.py:124
  60.5 0.5 fusion.1
  61.0 0.0 copy-start.5
  61.0 0.9 maximum_select_fusion.q_ref
  62.0 1.1 tile.5
  63.1 5.1 %all-to-all-start.1 = ((bf16[32,32,512]{2,1,0:T(8,128)(2,1)}), bf16[32,32,512]{2,1,0:T(8,128)(2,1)S(1)}, u32[]{:S(2)}, u32[]{:S(2)}) async-start(bf16[32,32,512]{2,1,0:T(8,128)(2,1)} %tile.5), calls=%async_computation.1 | async-start | bytes 2097152 | tf_op jit(solution)/shard_map/all_to_all | solution.py:121
  68.2 1.9 %collective-permute-start.5 = (bf16[2,2,256,1024]{3,2,1,0:T(8,128)(2,1)}, bf16[2,2,256,1024]{3,2,1,0:T(8,128)(2,1)}, u32[]{:S(2)}, u32[]{:S(2)}) collective-permute-start(bf16[2,2,256,1024]{3,2,1,0:T(8,128)(2,1)} %param.11), channel_id=1, source_target_pairs={{0,32},{1,33},{2,34},{3,35},{4,36},{5,37},{6,38},{7,39},{8,40},{9,... | collective-permute-start | bytes 6291464 | tf_op jit(solution)/shard_map/ppermute | solution.py:68
  70.1 3.7 %collective-permute-start.6 = (bf16[2,2,256,1024]{3,2,1,0:T(8,128)(2,1)}, bf16[2,2,256,1024]{3,2,1,0:T(8,128)(2,1)}, u32[]{:S(2)}, u32[]{:S(2)}) collective-permute-start(bf16[2,2,256,1024]{3,2,1,0:T(8,128)(2,1)} %param.11), channel_id=1, source_target_pairs={{32,0},{33,1},{34,2},{35,3},{36,4},{37,5},{38,6},{39,7},{40,8},{41... | collective-permute-start | bytes 6291464 | tf_op jit(solution)/shard_map/ppermute | solution.py:69
  74.5 0.7 collective-permute-start.2
  75.2 0.7 collective-permute-start.3
  76.0 0.7 collective-permute-start.4
  76.7 0.0 copy-done.5
  76.7 0.5 clamp_bitcast_fusion.slots_ref
  77.3 0.0 collective-permute-done.2
  77.3 0.0 collective-permute-done.3
  77.3 0.0 collective-permute-done.4
  77.3 1.6 %pad_maximum_fusion.1 = bf16[4,2,2,64,1024]{4,3,2,1,0:T(8,128)(2,1)} fusion(bf16[1,2,2,64,1024]{4,3,2,1,0:T(8,128)(2,1)S(1)} %bitcast.28, bf16[1,2,2,64,1024]{4,3,2,1,0:T(8,128)(2,1)S(1)} %bitcast.27, bf16[1,2,2,64,1024]{4,3,2,1,0:T(8,128)(2,1)S(1)} %bitcast.26, bf16[1,2,2,64,1024]{4,3,2,1,0:T(8,128)(2,1)S(1)} %bitcast.25), kind=kLoop, calls=%fused_computation.2 | loop fusion | flops 3145728 | bytes 4194304 | tf_op jit(solution)/shard_map/stack | solution.py:105
  78.9 2.3 %gather_fusion = bf16[4,2,2,64,1024]{4,3,2,1,0:T(8,128)(2,1)S(1)} fusion(bf16[4,2,2,64,1024]{4,3,2,1,0:T(8,128)(2,1)} %pad_maximum_fusion.1, s32[1024]{0:T(1024)S(1)} %pad_clamp_fusion), kind=kCustom, calls=%fused_computation | custom fusion | bytes 4194320 | tf_op jit(solution)/shard_map/jit(_take)/gather | solution.py:107
  81.1 16.8 %all-to-all-done.1 = bf16[32,32,512]{2,1,0:T(8,128)(2,1)S(1)} async-done(((bf16[32,32,512]{2,1,0:T(8,128)(2,1)}), bf16[32,32,512]{2,1,0:T(8,128)(2,1)S(1)}, u32[]{:S(2)}, u32[]{:S(2)}) %all-to-all-start.1) | async-done | bytes 1048608 | tf_op jit(solution)/shard_map/all_to_all | solution.py:121
  98.0 19.6 %collective-permute-start.7 = (bf16[1024,512]{1,0:T(8,128)(2,1)S(1)}, bf16[1024,512]{1,0:T(8,128)(2,1)}, u32[]{:S(2)}, u32[]{:S(2)}) collective-permute-start(bf16[1024,512]{1,0:T(8,128)(2,1)S(1)} %bitcast.21), channel_id=1, source_target_pairs={{0,32},{32,0},{64,96},{96,64},{128,160},{160,128},{192,224},{224,1... | collective-permute-start | bytes 3145736 | tf_op jit(solution)/shard_map/ppermute | solution.py:124
  117.6 0.3 select_bitcast_fusion
  117.8 0.3 copy.8
  118.1 0.0 collective-permute-done.5
  118.1 0.0 collective-permute-done.6
  118.1 2.6 %bitcast_select_fusion.1 = (bf16[2,2,256,1024]{3,2,1,0:T(8,128)(2,1)S(1)}, bf16[2,2,256,1024]{3,2,1,0:T(8,128)(2,1)S(1)}) fusion(bf16[2,2,256,1024]{3,2,1,0:T(8,128)(2,1)} %collective-permute-done.5, bf16[2,2,4,64,1024]{4,3,2,1,0:T(8,128)(2,1)S(1)} %copy.8, pred[]{:T(512)S(6)} %eq.17, bf16[2,2,256,1024]{3,2,1,0:T(8,128)(2,1)} %collective-permute-done.6, ...), kind=kLoop, calls=%fused_computation.4 | loop fusion | flops 2097152 | bytes 10485762 | tf_op jit(solution)/shard_map/jit(_where)/select_n | solution.py:109
  120.7 4.5 %pad_maximum_fusion.refs_0_.refs_1_.refs_2_.refs_3_.refs_4_.refs_5_.refs_6_.refs_7_ = bf16[2,6,256,1024]{3,2,1,0:T(8,128)(2,1)} fusion(bf16[2,2,256,1024]{3,2,1,0:T(8,128)(2,1)S(1)} %get-tuple-element.10, bf16[2,2,256,1024]{3,2,1,0:T(8,128)(2,1)} %param.11, bf16[2,2,256,1024]{3,2,1,0:T(8,128)(2,1)S(1)} %get-tuple-element.9), kind=kLoop, calls=%fused_computation.1 | loop fusion | flops 6291456 | bytes 12582912 | tf_op jit(solution)/shard_map/concatenate | solution.py:145
  125.3 12.0 %shard_map.73 = bf16[256,1024]{1,0:T(8,128)(2,1)} custom-call(s32[4]{0:T(128)} %clamp_bitcast_fusion.slots_ref, s32[1]{0:T(128)S(6)} %copy.9.count_ref, bf16[256,1024]{1,0:T(8,128)(2,1)} %maximum_select_fusion.q_ref, bf16[2,6,256,1024]{3,2,1,0:T(8,128)(2,1)} %pad_maximum_fusion.refs_0_.refs_1_.refs_2_.refs_3_.refs_4_.refs_5_.refs_6_.refs_7_, ...), custom_call_target="tpu_custom_call" | custom-call | tf_op jit(solution)/shard_map/pallas_call | solution.py:51
  137.3 0.0 copy-start.1
  137.3 0.0 collective-permute-done.7
  137.3 1.8 %fusion.5 = f32[256,1024]{1,0:T(8,128)S(1)} fusion(bf16[1024,512]{1,0:T(8,128)(2,1)} %collective-permute-done.7, bf16[256,1024]{1,0:T(8,128)(2,1)} %shard_map.73, s32[]{:T(128)S(6)} %select_n.111), kind=kOutput, calls=%fused_computation.17 | convolution fusion | flops 268435456 | bytes 2359300 | tf_op jit(solution)/shard_map/dot_general | solution.py:153
  139.1 0.0 copy-done.1
  139.1 1.3 add_convert_fusion
  (7 shorter events, 0.1 us)
Async XLA Ops:
  0.0 1.9 %copy-start = (bf16[32,1024]{1,0:T(8,128)(2,1)S(1)}, bf16[32,1024]{1,0:T(8,128)(2,1)}, u32[]{:S(2)}) copy-start(bf16[32,1024]{1,0:T(8,128)(2,1)} %param.9) | copy-start | bytes 196612
  0.0 58.3 %copy-start.4 = (bf16[1024]{0:T(1024)(128)(2,1)S(1)}, bf16[1024]{0:T(1024)(128)(2,1)}, u32[]{:S(2)}) copy-start(bf16[1024]{0:T(1024)(128)(2,1)} %param.8) | copy-start | bytes 6148
  0.0 58.3 %copy-start.3 = (bf16[1024,32]{0,1:T(8,128)(2,1)S(1)}, bf16[1024,32]{0,1:T(8,128)(2,1)}, u32[]{:S(2)}) copy-start(bf16[1024,32]{0,1:T(8,128)(2,1)} %param.10) | copy-start | bytes 196612
  0.0 58.3 %copy-start.2 = (bf16[256,1024]{1,0:T(8,128)(2,1)S(1)}, bf16[256,1024]{1,0:T(8,128)(2,1)}, u32[]{:S(2)}) copy-start(bf16[256,1024]{1,0:T(8,128)(2,1)} %param.7) | copy-start | bytes 1572868
  1.2 0.8 collective-permute-start
  32.1 28.5 %collective-permute-start.1 = (bf16[1024,512]{1,0:T(8,128)(2,1)S(1)}, bf16[1024,512]{1,0:T(8,128)(2,1)S(1)}, u32[]{:S(2)}, u32[]{:S(2)}) collective-permute-start(bf16[1024,512]{1,0:T(8,128)(2,1)S(1)} %bitcast.23), channel_id=1, source_target_pairs={{0,32},{32,0},{64,96},{96,64},{128,160},{160,128},{192,224},{224,1... | collective-permute-start | bytes 3145736 | tf_op jit(solution)/shard_map/ppermute | solution.py:124
  61.0 15.7 %copy-start.5 = (s32[1,4]{1,0:T(1,128)S(1)}, s32[1,4]{1,0:T(1,128)}, u32[]{:S(2)}) copy-start(s32[1,4]{1,0:T(1,128)} %param.12) | copy-start | bytes 52
  63.1 34.9 %all-to-all-start.1 = ((bf16[32,32,512]{2,1,0:T(8,128)(2,1)}), bf16[32,32,512]{2,1,0:T(8,128)(2,1)S(1)}, u32[]{:S(2)}, u32[]{:S(2)}) async-start(bf16[32,32,512]{2,1,0:T(8,128)(2,1)} %tile.5), calls=%async_computation.1 | async-start | bytes 2097152 | tf_op jit(solution)/shard_map/all_to_all | solution.py:121
  68.2 49.9 %collective-permute-start.5 = (bf16[2,2,256,1024]{3,2,1,0:T(8,128)(2,1)}, bf16[2,2,256,1024]{3,2,1,0:T(8,128)(2,1)}, u32[]{:S(2)}, u32[]{:S(2)}) collective-permute-start(bf16[2,2,256,1024]{3,2,1,0:T(8,128)(2,1)} %param.11), channel_id=1, source_target_pairs={{0,32},{1,33},{2,34},{3,35},{4,36},{5,37},{6,38},{7,39},{8,40},{9,... | collective-permute-start | bytes 6291464 | tf_op jit(solution)/shard_map/ppermute | solution.py:68
  70.1 48.0 %collective-permute-start.6 = (bf16[2,2,256,1024]{3,2,1,0:T(8,128)(2,1)}, bf16[2,2,256,1024]{3,2,1,0:T(8,128)(2,1)}, u32[]{:S(2)}, u32[]{:S(2)}) collective-permute-start(bf16[2,2,256,1024]{3,2,1,0:T(8,128)(2,1)} %param.11), channel_id=1, source_target_pairs={{32,0},{33,1},{34,2},{35,3},{36,4},{37,5},{38,6},{39,7},{40,8},{41... | collective-permute-start | bytes 6291464 | tf_op jit(solution)/shard_map/ppermute | solution.py:69
  74.5 2.7 %collective-permute-start.2 = (bf16[2,2,64,1024]{3,2,1,0:T(8,128)(2,1)S(1)}, bf16[2,2,64,1024]{3,2,1,0:T(8,128)(2,1)S(1)}, u32[]{:S(2)}, u32[]{:S(2)}) collective-permute-start(bf16[2,2,64,1024]{3,2,1,0:T(8,128)(2,1)S(1)} %collective-permute-done), channel_id=1, source_target_pairs={{224,252},{225,253},{226,254},{227,255},{228,224},{229,225},{230,2... | collective-permute-start | bytes 1572872 | tf_op jit(solution)/shard_map/ppermute | solution.py:94
  75.2 2.0 %collective-permute-start.3 = (bf16[2,2,64,1024]{3,2,1,0:T(8,128)(2,1)S(1)}, bf16[2,2,64,1024]{3,2,1,0:T(8,128)(2,1)S(1)}, u32[]{:S(2)}, u32[]{:S(2)}) collective-permute-start(bf16[2,2,64,1024]{3,2,1,0:T(8,128)(2,1)S(1)} %collective-permute-done), channel_id=1, source_target_pairs={{224,232},{225,233},{226,234},{227,235},{228,236},{229,237},{230,2... | collective-permute-start | bytes 1572872 | tf_op jit(solution)/shard_map/ppermute | solution.py:94
  76.0 1.3 collective-permute-start.4
  98.0 39.3 %collective-permute-start.7 = (bf16[1024,512]{1,0:T(8,128)(2,1)S(1)}, bf16[1024,512]{1,0:T(8,128)(2,1)}, u32[]{:S(2)}, u32[]{:S(2)}) collective-permute-start(bf16[1024,512]{1,0:T(8,128)(2,1)S(1)} %bitcast.21), channel_id=1, source_target_pairs={{0,32},{32,0},{64,96},{96,64},{128,160},{160,128},{192,224},{224,1... | collective-permute-start | bytes 3145736 | tf_op jit(solution)/shard_map/ppermute | solution.py:124
  137.3 1.8 %copy-start.1 = (bf16[256,1024]{1,0:T(8,128)(2,1)S(1)}, bf16[256,1024]{1,0:T(8,128)(2,1)}, u32[]{:S(2)}) copy-start(bf16[256,1024]{1,0:T(8,128)(2,1)} %shard_map.73) | copy-start | bytes 1572868

commit v5 on v1

--- a/solution.py
+++ b/solution.py
@@ -22,7 +22,7 @@
         scores = []
         for slot, key_ref in enumerate(key_refs):
             s = lax.dot_general(q_head, key_ref[...], (((1,), (1,)), ((), ())), preferred_element_type=jnp.float32)
-            scores.append(jnp.where(slot < count, s, -jnp.inf))
+            scores.append(s if slot == 0 else jnp.where(slot < count, s, -jnp.inf))
         peak = scores[0].max(axis=1, keepdims=True)
         for s in scores[1:]:
             peak = jnp.maximum(peak, s.max(axis=1, keepdims=True))
@@ -39,7 +39,7 @@
     out_ref[...] = result.astype(out_ref.dtype)
 
 
-def attend(q, window, slots, count, lanes=128):
+def attend(q, window, slots, count, lanes=256):
     rows, width = q.shape
     nbr = slots.shape[0]
     q_spec = pl.BlockSpec((rows, lanes), lambda h, s, c: (0, h))
@@ -79,13 +79,10 @@
     return below, above, own
 
 
-def far_side(kv, below, above, own):
+def far_side(own):
     lat_count, lon_count = lax.axis_size("lat"), lax.axis_size("lon")
-    lat, lon = lax.axis_index("lat"), lax.axis_index("lon")
     both = ("lat", "lon")
     split = lat_count // 2
-    rows = kv.shape[2] // Y_LO
-    z = lon // Y_LO
     z_count = lon_count // Y_LO
 
     def along_z(value, shift):
@@ -96,11 +93,16 @@
                 pairs.append((band * lon_count + l, band * lon_count + target))
         return lax.ppermute(value, both, pairs)
 
-    half = rows // 2
-    opposite = jnp.concatenate(
-        [along_z(own[:, :, :half], 2), along_z(own[:, :, half:], -2)], axis=2
-    )
-    quarters = jnp.stack([own, along_z(own, -1), opposite, along_z(own, 1)])
+    moved = [along_z(own, 2), along_z(own, -1), along_z(own, 1)]
+    return moved
+
+
+def assembled(kv, below, above, own, moved):
+    lat_count = lax.axis_size("lat")
+    lat, lon = lax.axis_index("lat"), lax.axis_index("lon")
+    split = lat_count // 2
+    z = lon // Y_LO
+    quarters = jnp.stack([own, moved[1], moved[0], moved[2]])
     order = (jnp.arange(Y_LO) - z) % Y_LO
     joined = jnp.take(quarters, order, axis=0)
     joined = jnp.moveaxis(joined, 0, 2).reshape(kv.shape)
@@ -140,7 +142,8 @@
     query = (projected * HD ** (-0.5)).astype(jnp.bfloat16)
     local_lists = nbr_lists - (lax.axis_index("lat") - 1) * blocks_here
     slots = jnp.clip(local_lists[0], 0, 3 * blocks_here - 1)
-    below, above = far_side(kv_cache, *sent)
+    moved = far_side(sent[2])
+    below, above = assembled(kv_cache, *sent, moved)
     window = jnp.concatenate([below, kv_cache, above], axis=1)
     attended = attend(query, window, slots, counts)
     w_out_rows = gathered_rows(w_out.T, after=query)

time: 143 us -> 138 us (0.965)
  the two profiles are of different devices: /device:TPU:57 before, /device:TPU:6 now
where the time goes in v5:
time: 138 us
  starting transfers between devices  52.5 us (38%)
  blocking collectives  31.7 us (23%)
  waiting for transfers between devices  21.9 us (16%)
  other arithmetic  11.4 us (8%)
  Pallas kernels  10.3 us (7%)
  local copies, waits for them, and re-layouts  5.73 us (4%)
  matrix products  3.09 us (2%)
    ppermute x2, starting transfers between devices, gathered_rows(): other = lax.ppermute(fetched, 'lat', swap)  38.7 us
    all_to_all x1, blocking collectives, gathered_rows(): lax.all_to_all(jnp.tile(mine, (lon_count, 1)), 'lon', 0, 0, tiled=True)  31.7 us
    all_to_all x1, waiting for transfers between devices, gathered_rows(): lax.all_to_all(jnp.tile(mine, (lon_count, 1)), 'lon', 0, 0, tiled=True)  19.9 us
    pallas_call x1, Pallas kernels, attend(): pl.pallas_call(attention_kernel, grid_spec=pltpu.PrefetchScalarGridSpec(n...  10.3 us
    all_to_all x1, starting transfers between devices, gathered_rows(): lax.all_to_all(jnp.tile(mine, (lon_count, 1)), 'lon', 0, 0, tiled=True)  5.51 us
    concatenate x1, other arithmetic, layer(): window = jnp.concatenate([below, kv_cache, above], axis=1)  4.55 us
    ppermute x1, starting transfers between devices, neighbour_bands(): above = lax.ppermute(kv, both, [(j, i) for i, j in up])  3.56 us
  transfers between devices with their start and end apart: 9, of which 2 were waited for; matrix products, arithmetic and copies ran while one was open for 9% of the time, Pallas kernels for 8%

profile of v5, /device:TPU:6, one launch (start us, length us, event | category | flops | bytes accessed | tf_op | source)
XLA Modules:
  0.0 137.6 jit_solution(3252300465291294919)
XLA Ops:
  0.0 0.0 copy-start
  0.0 0.0 copy-start.6
  0.0 0.0 copy-start.5
  0.0 0.0 copy-start.2
  0.0 1.1 constant_dynamic-slice_fusion
  1.2 0.7 collective-permute-start
  1.9 0.0 copy-done
  1.9 0.0 collective-permute-done
  1.9 0.0 copy-start.3
  1.9 0.8 copy-done.3
  2.7 0.1 tile.4
  2.8 31.7 %all_to_all.18 = bf16[32,32,512]{2,1,0:T(8,128)(2,1)S(1)} all-to-all(bf16[32,32,512]{2,1,0:T(8,128)(2,1)S(1)} %tile.4), channel_id=1, replica_groups=mesh['lat'=16,'lon'=32] {'lon'}, dimensions={0} | all-to-all | bytes 2097152 | tf_op jit(solution)/shard_map/all_to_all | solution.py:121
  34.5 22.6 %collective-permute-start.1 = (bf16[1024,512]{1,0:T(8,128)(2,1)S(1)}, bf16[1024,512]{1,0:T(8,128)(2,1)S(1)}, u32[]{:S(2)}, u32[]{:S(2)}) collective-permute-start(bf16[1024,512]{1,0:T(8,128)(2,1)S(1)} %bitcast.23), channel_id=1, source_target_pairs={{0,32},{32,0},{64,96},{96,64},{128,160},{160,128},{192,224},{224,1... | collective-permute-start | bytes 3145736 | tf_op jit(solution)/shard_map/ppermute | solution.py:124
  57.1 0.0 copy-done.6
  57.2 0.0 copy-done.5
  57.2 0.0 copy-done.2
  57.2 0.2 fusion.17
  57.4 2.0 %collective-permute-done.1 = bf16[1024,512]{1,0:T(8,128)(2,1)S(1)} collective-permute-done((bf16[1024,512]{1,0:T(8,128)(2,1)S(1)}, bf16[1024,512]{1,0:T(8,128)(2,1)S(1)}, u32[]{:S(2)}, u32[]{:S(2)}) %collective-permute-start.1) | collective-permute-done | bytes 1048608 | tf_op jit(solution)/shard_map/ppermute | solution.py:124
  59.4 0.2 broadcast_select_fusion.3
  59.6 1.6 %fusion.11.q_ref = bf16[256,1024]{1,0:T(8,128)(2,1)} fusion(bf16[1024,512]{1,0:T(8,128)(2,1)S(1)} %get-tuple-element.14, bf16[1024,512]{1,0:T(8,128)(2,1)S(1)} %get-tuple-element.13, bf16[256,1024]{1,0:T(8,128)(2,1)S(1)} %copy-done.2, f32[1024]{0:T(1024)S(1)} %convert_element_type.16, f32[256]{0:T(256)S(1)} %add_rsqrt_fusion), kind=kOutput, calls=%fused_computation.17 | convolution fusion | flops 542638080 | bytes 3150848 | tf_op jit(solution)/shard_map/dot_general | solution.py:137
  61.2 1.1 tile.5
  62.3 5.5 %all-to-all-start.1 = ((bf16[32,32,512]{2,1,0:T(8,128)(2,1)}), bf16[32,32,512]{2,1,0:T(8,128)(2,1)S(1)}, u32[]{:S(2)}, u32[]{:S(2)}) async-start(bf16[32,32,512]{2,1,0:T(8,128)(2,1)} %tile.5), calls=%async_computation.1 | async-start | bytes 2097152 | tf_op jit(solution)/shard_map/all_to_all | solution.py:121
  67.8 2.0 %collective-permute-start.5 = (bf16[2,2,256,1024]{3,2,1,0:T(8,128)(2,1)}, bf16[2,2,256,1024]{3,2,1,0:T(8,128)(2,1)}, u32[]{:S(2)}, u32[]{:S(2)}) collective-permute-start(bf16[2,2,256,1024]{3,2,1,0:T(8,128)(2,1)} %param.11), channel_id=1, source_target_pairs={{0,32},{1,33},{2,34},{3,35},{4,36},{5,37},{6,38},{7,39},{8,40},{9,... | collective-permute-start | bytes 6291464 | tf_op jit(solution)/shard_map/ppermute | solution.py:68
  69.8 3.6 %collective-permute-start.6 = (bf16[2,2,256,1024]{3,2,1,0:T(8,128)(2,1)}, bf16[2,2,256,1024]{3,2,1,0:T(8,128)(2,1)}, u32[]{:S(2)}, u32[]{:S(2)}) collective-permute-start(bf16[2,2,256,1024]{3,2,1,0:T(8,128)(2,1)} %param.11), channel_id=1, source_target_pairs={{32,0},{33,1},{34,2},{35,3},{36,4},{37,5},{38,6},{39,7},{40,8},{41... | collective-permute-start | bytes 6291464 | tf_op jit(solution)/shard_map/ppermute | solution.py:69
  74.0 0.0 copy-done.4
  74.0 0.7 collective-permute-start.2
  74.7 0.7 collective-permute-start.3
  75.4 0.7 collective-permute-start.4
  76.2 0.0 copy-done.7
  76.2 0.5 clamp_bitcast_fusion.slots_ref
  76.7 0.0 collective-permute-done.2
  76.7 0.0 collective-permute-done.3
  76.7 0.0 collective-permute-done.4
  76.7 1.6 %pad_maximum_fusion.1 = bf16[4,2,2,64,1024]{4,3,2,1,0:T(8,128)(2,1)} fusion(bf16[1,2,2,64,1024]{4,3,2,1,0:T(8,128)(2,1)S(1)} %bitcast.27, bf16[1,2,2,64,1024]{4,3,2,1,0:T(8,128)(2,1)S(1)} %bitcast.26, bf16[1,2,2,64,1024]{4,3,2,1,0:T(8,128)(2,1)S(1)} %bitcast.25, bf16[1,2,2,64,1024]{4,3,2,1,0:T(8,128)(2,1)S(1)} %bitcast.24), kind=kLoop, calls=%fused_computation.6 | loop fusion | flops 3145728 | bytes 4194304 | tf_op jit(solution)/shard_map/stack | solution.py:105
  78.4 2.3 %gather_fusion = bf16[4,2,2,64,1024]{4,3,2,1,0:T(8,128)(2,1)S(1)} fusion(bf16[4,2,2,64,1024]{4,3,2,1,0:T(8,128)(2,1)} %pad_maximum_fusion.1, s32[1024]{0:T(1024)S(1)} %pad_clamp_fusion), kind=kCustom, calls=%fused_computation | custom fusion | bytes 4194320 | tf_op jit(solution)/shard_map/jit(_take)/gather | solution.py:107
  80.6 19.9 %all-to-all-done.1 = bf16[32,32,512]{2,1,0:T(8,128)(2,1)S(1)} async-done(((bf16[32,32,512]{2,1,0:T(8,128)(2,1)}), bf16[32,32,512]{2,1,0:T(8,128)(2,1)S(1)}, u32[]{:S(2)}, u32[]{:S(2)}) %all-to-all-start.1) | async-done | bytes 1048608 | tf_op jit(solution)/shard_map/all_to_all | solution.py:121
  100.5 16.1 %collective-permute-start.7 = (bf16[1024,512]{1,0:T(8,128)(2,1)S(1)}, bf16[1024,512]{1,0:T(8,128)(2,1)}, u32[]{:S(2)}, u32[]{:S(2)}) collective-permute-start(bf16[1024,512]{1,0:T(8,128)(2,1)S(1)} %bitcast.22), channel_id=1, source_target_pairs={{0,32},{32,0},{64,96},{96,64},{128,160},{160,128},{192,224},{224,1... | collective-permute-start | bytes 3145736 | tf_op jit(solution)/shard_map/ppermute | solution.py:124
  116.6 0.3 select_bitcast_fusion
  116.9 0.3 copy.8
  117.1 0.0 collective-permute-done.5
  117.1 0.0 collective-permute-done.6
  117.2 2.6 %bitcast_select_fusion.1 = (bf16[2,2,256,1024]{3,2,1,0:T(8,128)(2,1)S(1)}, bf16[2,2,256,1024]{3,2,1,0:T(8,128)(2,1)S(1)}) fusion(bf16[2,2,256,1024]{3,2,1,0:T(8,128)(2,1)} %collective-permute-done.5, bf16[2,2,4,64,1024]{4,3,2,1,0:T(8,128)(2,1)S(1)} %copy.8, pred[]{:T(512)S(6)} %eq.19, bf16[2,2,256,1024]{3,2,1,0:T(8,128)(2,1)} %collective-permute-done.6, ...), kind=kLoop, calls=%fused_computation.12 | loop fusion | flops 2097152 | bytes 10485762 | tf_op jit(solution)/shard_map/jit(_where)/select_n | solution.py:109
  119.8 4.5 %pad_maximum_fusion.refs_0_.refs_1_.refs_2_.refs_3_.refs_4_.refs_5_.refs_6_.refs_7_ = bf16[2,6,256,1024]{3,2,1,0:T(8,128)(2,1)} fusion(bf16[2,2,256,1024]{3,2,1,0:T(8,128)(2,1)S(1)} %get-tuple-element.12, bf16[2,2,256,1024]{3,2,1,0:T(8,128)(2,1)} %param.11, bf16[2,2,256,1024]{3,2,1,0:T(8,128)(2,1)S(1)} %get-tuple-element.11), kind=kLoop, calls=%fused_computation.1 | loop fusion | flops 6291456 | bytes 12582912 | tf_op jit(solution)/shard_map/concatenate | solution.py:147
  124.3 10.3 %shard_map.73 = bf16[256,1024]{1,0:T(8,128)(2,1)} custom-call(s32[4]{0:T(128)} %clamp_bitcast_fusion.slots_ref, s32[1]{0:T(128)S(6)} %copy.9.count_ref, bf16[256,1024]{1,0:T(8,128)(2,1)} %fusion.11.q_ref, bf16[2,6,256,1024]{3,2,1,0:T(8,128)(2,1)} %pad_maximum_fusion.refs_0_.refs_1_.refs_2_.refs_3_.refs_4_.refs_5_.refs_6_.refs_7_, ...), custom_call_target="tpu_custom_call" | custom-call | tf_op jit(solution)/shard_map/pallas_call | solution.py:51
  134.7 0.0 collective-permute-done.7
  134.7 1.4 %broadcast_select_fusion.1 = (bf16[1024,512]{1,0:T(8,128)(2,1)S(1)}, bf16[1024,512]{1,0:T(8,128)(2,1)S(1)}) fusion(bf16[1024,512]{1,0:T(8,128)(2,1)} %collective-permute-done.7, pred[]{:T(512)S(6)} %eq.18, bf16[32,32,512]{2,1,0:T(8,128)(2,1)S(1)} %all-to-all-done.1), kind=kLoop, calls=%fused_computation.23 | loop fusion | flops 1048576 | bytes 4194305 | tf_op jit(solution)/shard_map/jit(_where)/select_n | solution.py:125
  136.1 0.0 copy-done.1
  136.1 1.5 %fusion.14 = bf16[256,1024]{1,0:T(8,128)(2,1)} fusion(bf16[256,1024]{1,0:T(8,128)(2,1)S(1)} %copy-done.1, bf16[1024,512]{1,0:T(8,128)(2,1)S(1)} %get-tuple-element.10, bf16[1024,512]{1,0:T(8,128)(2,1)S(1)} %get-tuple-element.9), kind=kOutput, calls=%fused_computation.18 | convolution fusion | flops 541327360 | bytes 3145728 | tf_op jit(solution)/shard_map/dot_general | solution.py:150
  (10 shorter events, 0.1 us)
Async XLA Ops:
  0.0 1.9 %copy-start = (bf16[32,1024]{1,0:T(8,128)(2,1)S(1)}, bf16[32,1024]{1,0:T(8,128)(2,1)}, u32[]{:S(2)}) copy-start(bf16[32,1024]{1,0:T(8,128)(2,1)} %param.9) | copy-start | bytes 196612
  0.0 57.1 %copy-start.6 = (bf16[1024]{0:T(1024)(128)(2,1)S(1)}, bf16[1024]{0:T(1024)(128)(2,1)}, u32[]{:S(2)}) copy-start(bf16[1024]{0:T(1024)(128)(2,1)} %param.8) | copy-start | bytes 6148
  0.0 57.2 %copy-start.5 = (bf16[1024,32]{0,1:T(8,128)(2,1)S(1)}, bf16[1024,32]{0,1:T(8,128)(2,1)}, u32[]{:S(2)}) copy-start(bf16[1024,32]{0,1:T(8,128)(2,1)} %param.10) | copy-start | bytes 196612
  0.0 57.2 %copy-start.2 = (bf16[256,1024]{1,0:T(8,128)(2,1)S(1)}, bf16[256,1024]{1,0:T(8,128)(2,1)}, u32[]{:S(2)}) copy-start(bf16[256,1024]{1,0:T(8,128)(2,1)} %param.7) | copy-start | bytes 1572868
  1.2 0.8 collective-permute-start
  1.9 0.8 copy-start.3
  34.5 24.9 %collective-permute-start.1 = (bf16[1024,512]{1,0:T(8,128)(2,1)S(1)}, bf16[1024,512]{1,0:T(8,128)(2,1)S(1)}, u32[]{:S(2)}, u32[]{:S(2)}) collective-permute-start(bf16[1024,512]{1,0:T(8,128)(2,1)S(1)} %bitcast.23), channel_id=1, source_target_pairs={{0,32},{32,0},{64,96},{96,64},{128,160},{160,128},{192,224},{224,1... | collective-permute-start | bytes 3145736 | tf_op jit(solution)/shard_map/ppermute | solution.py:124
  61.2 12.9 %copy-start.4 = (bf16[2,2,64,1024]{3,2,1,0:T(8,128)(2,1)S(1)}, bf16[2,2,64,1024]{3,2,1,0:T(8,128)(2,1)}, u32[]{:S(2)}) copy-start(bf16[2,2,64,1024]{3,2,1,0:T(8,128)(2,1)} %copy-done.3) | copy-start | bytes 1572868
  61.2 15.0 %copy-start.7 = (s32[1,4]{1,0:T(1,128)S(1)}, s32[1,4]{1,0:T(1,128)}, u32[]{:S(2)}) copy-start(s32[1,4]{1,0:T(1,128)} %param.12) | copy-start | bytes 52
  62.3 38.3 %all-to-all-start.1 = ((bf16[32,32,512]{2,1,0:T(8,128)(2,1)}), bf16[32,32,512]{2,1,0:T(8,128)(2,1)S(1)}, u32[]{:S(2)}, u32[]{:S(2)}) async-start(bf16[32,32,512]{2,1,0:T(8,128)(2,1)} %tile.5), calls=%async_computation.1 | async-start | bytes 2097152 | tf_op jit(solution)/shard_map/all_to_all | solution.py:121
  67.8 49.4 %collective-permute-start.5 = (bf16[2,2,256,1024]{3,2,1,0:T(8,128)(2,1)}, bf16[2,2,256,1024]{3,2,1,0:T(8,128)(2,1)}, u32[]{:S(2)}, u32[]{:S(2)}) collective-permute-start(bf16[2,2,256,1024]{3,2,1,0:T(8,128)(2,1)} %param.11), channel_id=1, source_target_pairs={{0,32},{1,33},{2,34},{3,35},{4,36},{5,37},{6,38},{7,39},{8,40},{9,... | collective-permute-start | bytes 6291464 | tf_op jit(solution)/shard_map/ppermute | solution.py:68
  69.8 47.3 %collective-permute-start.6 = (bf16[2,2,256,1024]{3,2,1,0:T(8,128)(2,1)}, bf16[2,2,256,1024]{3,2,1,0:T(8,128)(2,1)}, u32[]{:S(2)}, u32[]{:S(2)}) collective-permute-start(bf16[2,2,256,1024]{3,2,1,0:T(8,128)(2,1)} %param.11), channel_id=1, source_target_pairs={{32,0},{33,1},{34,2},{35,3},{36,4},{37,5},{38,6},{39,7},{40,8},{41... | collective-permute-start | bytes 6291464 | tf_op jit(solution)/shard_map/ppermute | solution.py:69
  74.0 2.7 %collective-permute-start.2 = (bf16[2,2,64,1024]{3,2,1,0:T(8,128)(2,1)S(1)}, bf16[2,2,64,1024]{3,2,1,0:T(8,128)(2,1)S(1)}, u32[]{:S(2)}, u32[]{:S(2)}) collective-permute-start(bf16[2,2,64,1024]{3,2,1,0:T(8,128)(2,1)S(1)} %copy-done.4), channel_id=1, source_target_pairs={{224,252},{225,253},{226,254},{227,255},{228,224},{229,225},{230,2... | collective-permute-start | bytes 1572872 | tf_op jit(solution)/shard_map/ppermute | solution.py:94
  74.7 2.0 %collective-permute-start.3 = (bf16[2,2,64,1024]{3,2,1,0:T(8,128)(2,1)S(1)}, bf16[2,2,64,1024]{3,2,1,0:T(8,128)(2,1)S(1)}, u32[]{:S(2)}, u32[]{:S(2)}) collective-permute-start(bf16[2,2,64,1024]{3,2,1,0:T(8,128)(2,1)S(1)} %copy-done.4), channel_id=1, source_target_pairs={{224,232},{225,233},{226,234},{227,235},{228,236},{229,237},{230,2... | collective-permute-start | bytes 1572872 | tf_op jit(solution)/shard_map/ppermute | solution.py:94
  75.4 1.3 collective-permute-start.4
  100.5 34.1 %collective-permute-start.7 = (bf16[1024,512]{1,0:T(8,128)(2,1)S(1)}, bf16[1024,512]{1,0:T(8,128)(2,1)}, u32[]{:S(2)}, u32[]{:S(2)}) collective-permute-start(bf16[1024,512]{1,0:T(8,128)(2,1)S(1)} %bitcast.22), channel_id=1, source_target_pairs={{0,32},{32,0},{64,96},{96,64},{128,160},{160,128},{192,224},{224,1... | collective-permute-start | bytes 3145736 | tf_op jit(solution)/shard_map/ppermute | solution.py:124
  134.7 1.4 %copy-start.1 = (bf16[256,1024]{1,0:T(8,128)(2,1)S(1)}, bf16[256,1024]{1,0:T(8,128)(2,1)}, u32[]{:S(2)}) copy-start(bf16[256,1024]{1,0:T(8,128)(2,1)} %shard_map.73) | copy-start | bytes 1572868

commit v6 on v5

--- a/solution.py
+++ b/solution.py
@@ -22,7 +22,7 @@
         scores = []
         for slot, key_ref in enumerate(key_refs):
             s = lax.dot_general(q_head, key_ref[...], (((1,), (1,)), ((), ())), preferred_element_type=jnp.float32)
-            scores.append(s if slot == 0 else jnp.where(slot < count, s, -jnp.inf))
+            scores.append(jnp.where(slot < count, s, -jnp.inf))
         peak = scores[0].max(axis=1, keepdims=True)
         for s in scores[1:]:
             peak = jnp.maximum(peak, s.max(axis=1, keepdims=True))
@@ -97,15 +97,12 @@
     return moved
 
 
-def assembled(kv, below, above, own, moved):
+def assembled(below, above, own, moved):
     lat_count = lax.axis_size("lat")
     lat, lon = lax.axis_index("lat"), lax.axis_index("lon")
     split = lat_count // 2
     z = lon // Y_LO
-    quarters = jnp.stack([own, moved[1], moved[0], moved[2]])
-    order = (jnp.arange(Y_LO) - z) % Y_LO
-    joined = jnp.take(quarters, order, axis=0)
-    joined = jnp.moveaxis(joined, 0, 2).reshape(kv.shape)
+    joined = jnp.roll(jnp.concatenate([own, moved[1], moved[0], moved[2]], axis=2), z * own.shape[2], axis=2)
     below = jnp.where(lat == split, joined, below)
     above = jnp.where(lat == split - 1, joined, above)
     return below, above
@@ -143,7 +140,7 @@
     local_lists = nbr_lists - (lax.axis_index("lat") - 1) * blocks_here
     slots = jnp.clip(local_lists[0], 0, 3 * blocks_here - 1)
     moved = far_side(sent[2])
-    below, above = assembled(kv_cache, *sent, moved)
+    below, above = assembled(*sent, moved)
     window = jnp.concatenate([below, kv_cache, above], axis=1)
     attended = attend(query, window, slots, counts)
     w_out_rows = gathered_rows(w_out.T, after=query)

time: 138 us -> 144 us (1.043)
  local copies, waits for them, and re-layouts: 5.73 us -> 16.4 us
  waiting for transfers between devices: 21.9 us -> 15 us
    unnamed x16 -> x27, local copies, waits for them, and re-layouts: 0.82 us -> 12 us
    all_to_all x1, waiting for transfers between devices: 19.9 us -> 13 us  [gathered_rows(): lax.all_to_all(jnp.tile(mine, (lon_count, 1)), 'lon', 0, 0, tiled=True)]
    gather x1 -> x0, local copies, waits for them, and re-layouts: 2.27 us -> none  [assembled(): joined = jnp.take(quarters, order, axis=0)]
    concatenate x0 -> x1, local copies, waits for them, and re-layouts: none -> 1.9 us  [assembled(): jnp.roll(jnp.concatenate([own, moved[1], moved[0], moved[2]], axis=2), z...]
    select_n x1, other arithmetic: 2.61 us -> 4.5 us  [assembled(): below = jnp.where(lat == split, joined, below)]
    ppermute x3, starting transfers between devices: 2.08 us -> 3.74 us  [along_z(): return lax.ppermute(value, both, pairs)]
    another operation x1 -> x0, other arithmetic: 1.63 us -> none  [assembled(): quarters = jnp.stack([own, moved[1], moved[0], moved[2]])]
  transfers between devices with their start and end apart: 9 -> 9, of which waited for: 2 -> 2; matrix products, arithmetic and copies ran while one was open for 9% -> 16% of each run, Pallas kernels for 8% -> 7%
where the time goes in v6:
time: 144 us; the launch traced here: 143 us
  starting transfers between devices  53.9 us (37%)
  blocking collectives  31.7 us (22%)
  local copies, waits for them, and re-layouts  16.4 us (11%)
  waiting for transfers between devices  15 us (10%)
  other arithmetic  11.8 us (8%)
  Pallas kernels  10.5 us (7%)
  matrix products  3.1 us (2%)
    ppermute x2, starting transfers between devices, gathered_rows(): other = lax.ppermute(fetched, 'lat', swap)  38.4 us
    all_to_all x1, blocking collectives, gathered_rows(): lax.all_to_all(jnp.tile(mine, (lon_count, 1)), 'lon', 0, 0, tiled=True)  31.7 us
    all_to_all x1, waiting for transfers between devices, gathered_rows(): lax.all_to_all(jnp.tile(mine, (lon_count, 1)), 'lon', 0, 0, tiled=True)  13 us
    unnamed x27, local copies, waits for them, and re-layouts  12 us
    pallas_call x1, Pallas kernels, attend(): pl.pallas_call(attention_kernel, grid_spec=pltpu.PrefetchScalarGridSpec(n...  10.5 us
    all_to_all x1, starting transfers between devices, gathered_rows(): lax.all_to_all(jnp.tile(mine, (lon_count, 1)), 'lon', 0, 0, tiled=True)  5.5 us
    concatenate x1, other arithmetic, layer(): window = jnp.concatenate([below, kv_cache, above], axis=1)  5.01 us
    select_n x1, other arithmetic, assembled(): below = jnp.where(lat == split, joined, below)  4.5 us
  transfers between devices with their start and end apart: 9, of which 2 were waited for; matrix products, arithmetic and copies ran while one was open for 16% of the time, Pallas kernels for 7%

profile of v6, /device:TPU:6, one launch (start us, length us, event | category | flops | bytes accessed | tf_op | source)
XLA Modules:
  0.0 143.3 jit_solution(5122223124407044022)
XLA Ops:
  0.0 0.0 copy-start
  0.0 0.0 copy-start.6
  0.1 1.2 constant_dynamic-slice_fusion
  1.2 0.7 collective-permute-start
  1.9 0.0 copy-done
  2.0 0.0 collective-permute-done
  2.0 0.0 copy-start.2
  2.0 0.8 copy-done.2
  2.8 0.1 tile.4
  2.9 31.7 %all_to_all.18 = bf16[32,32,512]{2,1,0:T(8,128)(2,1)S(1)} all-to-all(bf16[32,32,512]{2,1,0:T(8,128)(2,1)S(1)} %tile.4), channel_id=1, replica_groups=mesh['lat'=16,'lon'=32] {'lon'}, dimensions={0} | all-to-all | bytes 2097152 | tf_op jit(solution)/shard_map/all_to_all | solution.py:118
  34.6 22.6 %collective-permute-start.1 = (bf16[1024,512]{1,0:T(8,128)(2,1)S(1)}, bf16[1024,512]{1,0:T(8,128)(2,1)S(1)}, u32[]{:S(2)}, u32[]{:S(2)}) collective-permute-start(bf16[1024,512]{1,0:T(8,128)(2,1)S(1)} %bitcast.12), channel_id=1, source_target_pairs={{0,32},{32,0},{64,96},{96,64},{128,160},{160,128},{192,224},{224,1... | collective-permute-start | bytes 3145736 | tf_op jit(solution)/shard_map/ppermute | solution.py:121
  57.2 0.0 copy-done.8
  57.3 0.2 fusion.17
  57.5 2.0 %collective-permute-done.1 = bf16[1024,512]{1,0:T(8,128)(2,1)S(1)} collective-permute-done((bf16[1024,512]{1,0:T(8,128)(2,1)S(1)}, bf16[1024,512]{1,0:T(8,128)(2,1)S(1)}, u32[]{:S(2)}, u32[]{:S(2)}) %collective-permute-start.1) | collective-permute-done | bytes 1048608 | tf_op jit(solution)/shard_map/ppermute | solution.py:121
  59.5 0.2 broadcast_select_fusion.5
  59.7 0.0 copy-start.1
  59.7 0.0 copy-start.9
  59.7 1.6 %fusion.11.q_ref = bf16[256,1024]{1,0:T(8,128)(2,1)} fusion(bf16[1024,512]{1,0:T(8,128)(2,1)S(1)} %get-tuple-element.14, bf16[1024,512]{1,0:T(8,128)(2,1)S(1)} %get-tuple-element.13, bf16[256,1024]{1,0:T(8,128)(2,1)S(1)} %copy-done.6, f32[1024]{0:T(1024)S(1)} %convert_element_type.16, f32[256]{0:T(256)S(1)} %add_rsqrt_fusion), kind=kOutput, calls=%fused_computation.14 | convolution fusion | flops 542638080 | bytes 3150848 | tf_op jit(solution)/shard_map/dot_general | solution.py:134
  61.3 1.2 tile.5
  62.5 5.5 %all-to-all-start.1 = ((bf16[32,32,512]{2,1,0:T(8,128)(2,1)}), bf16[32,32,512]{2,1,0:T(8,128)(2,1)S(1)}, u32[]{:S(2)}, u32[]{:S(2)}) async-start(bf16[32,32,512]{2,1,0:T(8,128)(2,1)} %tile.5), calls=%async_computation.1 | async-start | bytes 2097152 | tf_op jit(solution)/shard_map/all_to_all | solution.py:118
  68.0 2.0 %collective-permute-start.5 = (bf16[2,2,256,1024]{3,2,1,0:T(8,128)(2,1)S(1)}, bf16[2,2,256,1024]{3,2,1,0:T(8,128)(2,1)}, u32[]{:S(2)}, u32[]{:S(2)}) collective-permute-start(bf16[2,2,256,1024]{3,2,1,0:T(8,128)(2,1)S(1)} %copy-done.1), channel_id=1, source_target_pairs={{0,32},{1,33},{2,34},{3,35},{4,36},{5,37},{6,38},{7,39},{8,40},{9,... | collective-permute-start | bytes 6291464 | tf_op jit(solution)/shard_map/ppermute | solution.py:68
  70.0 3.5 %collective-permute-start.6 = (bf16[2,2,256,1024]{3,2,1,0:T(8,128)(2,1)S(1)}, bf16[2,2,256,1024]{3,2,1,0:T(8,128)(2,1)}, u32[]{:S(2)}, u32[]{:S(2)}) collective-permute-start(bf16[2,2,256,1024]{3,2,1,0:T(8,128)(2,1)S(1)} %copy-done.1), channel_id=1, source_target_pairs={{32,0},{33,1},{34,2},{35,3},{36,4},{37,5},{38,6},{39,7},{40,8},{41... | collective-permute-start | bytes 6291464 | tf_op jit(solution)/shard_map/ppermute | solution.py:69
  73.5 1.5 %collective-permute-start.2 = (bf16[2,2,64,1024]{3,2,1,0:T(8,128)(2,1)}, bf16[2,2,64,1024]{3,2,1,0:T(8,128)(2,1)}, u32[]{:S(2)}, u32[]{:S(2)}) collective-permute-start(bf16[2,2,64,1024]{3,2,1,0:T(8,128)(2,1)} %copy-done.2), channel_id=1, source_target_pairs={{224,252},{225,253},{226,254},{227,255},{228,224},{229,225},{230,2... | collective-permute-start | bytes 1572872 | tf_op jit(solution)/shard_map/ppermute | solution.py:94
  75.0 1.5 %collective-permute-start.3 = (bf16[2,2,64,1024]{3,2,1,0:T(8,128)(2,1)}, bf16[2,2,64,1024]{3,2,1,0:T(8,128)(2,1)}, u32[]{:S(2)}, u32[]{:S(2)}) collective-permute-start(bf16[2,2,64,1024]{3,2,1,0:T(8,128)(2,1)} %copy-done.2), channel_id=1, source_target_pairs={{224,232},{225,233},{226,234},{227,235},{228,236},{229,237},{230,2... | collective-permute-start | bytes 1572872 | tf_op jit(solution)/shard_map/ppermute | solution.py:94
  77.1 0.8 collective-permute-start.4
  78.0 0.5 clamp_bitcast_fusion.slots_ref
  78.5 1.9 %constant_dynamic-update-slice_fusion.7 = bf16[2,2,512,1024]{3,2,1,0:T(8,128)(2,1)} fusion(bf16[2,2,64,1024]{3,2,1,0:T(8,128)(2,1)} %copy-done.2), kind=kLoop, calls=%fused_computation.33 | loop fusion | bytes 1048576
  80.3 0.0 collective-permute-done.2
  80.3 1.9 %constant_dynamic-update-slice_fusion.6 = bf16[2,2,512,1024]{3,2,1,0:T(8,128)(2,1)} fusion(bf16[2,2,512,1024]{3,2,1,0:T(8,128)(2,1)} %constant_dynamic-update-slice_fusion.7, bf16[2,2,64,1024]{3,2,1,0:T(8,128)(2,1)} %collective-permute-done.2), kind=kLoop, calls=%fused_computation.32 | loop fusion | bytes 1048576
  82.2 0.0 collective-permute-done.3
  82.2 1.9 %constant_dynamic-update-slice_fusion.5 = bf16[2,2,512,1024]{3,2,1,0:T(8,128)(2,1)} fusion(bf16[2,2,512,1024]{3,2,1,0:T(8,128)(2,1)} %constant_dynamic-update-slice_fusion.6, bf16[2,2,64,1024]{3,2,1,0:T(8,128)(2,1)} %collective-permute-done.3), kind=kLoop, calls=%fused_computation.31 | loop fusion | bytes 1048576
  84.1 0.0 collective-permute-done.4
  84.1 0.9 constant_dynamic-update-slice_fusion.4
  85.0 0.9 constant_dynamic-update-slice_fusion.3
  85.9 0.0 copy-done.4
  85.9 1.9 %constant_dynamic-update-slice_fusion.2 = bf16[2,2,512,1024]{3,2,1,0:T(8,128)(2,1)} fusion(bf16[2,2,512,1024]{3,2,1,0:T(8,128)(2,1)} %constant_dynamic-update-slice_fusion.3, bf16[2,2,64,1024]{3,2,1,0:T(8,128)(2,1)} %collective-permute-done.2), kind=kLoop, calls=%fused_computation.28 | loop fusion | bytes 1048576
  87.8 13.0 %all-to-all-done.1 = bf16[32,32,512]{2,1,0:T(8,128)(2,1)S(1)} async-done(((bf16[32,32,512]{2,1,0:T(8,128)(2,1)}), bf16[32,32,512]{2,1,0:T(8,128)(2,1)S(1)}, u32[]{:S(2)}, u32[]{:S(2)}) %all-to-all-start.1) | async-done | bytes 1048608 | tf_op jit(solution)/shard_map/all_to_all | solution.py:118
  100.8 15.8 %collective-permute-start.7 = (bf16[1024,512]{1,0:T(8,128)(2,1)S(1)}, bf16[1024,512]{1,0:T(8,128)(2,1)}, u32[]{:S(2)}, u32[]{:S(2)}) collective-permute-start(bf16[1024,512]{1,0:T(8,128)(2,1)S(1)} %bitcast.11), channel_id=1, source_target_pairs={{0,32},{32,0},{64,96},{96,64},{128,160},{160,128},{192,224},{224,1... | collective-permute-start | bytes 3145736 | tf_op jit(solution)/shard_map/ppermute | solution.py:121
  116.6 1.9 %constant_dynamic-update-slice_fusion.1 = bf16[2,2,512,1024]{3,2,1,0:T(8,128)(2,1)} fusion(bf16[2,2,512,1024]{3,2,1,0:T(8,128)(2,1)} %constant_dynamic-update-slice_fusion.2, bf16[2,2,64,1024]{3,2,1,0:T(8,128)(2,1)} %collective-permute-done.3), kind=kLoop, calls=%fused_computation.27 | loop fusion | bytes 1048576
  118.4 1.9 %constant_dynamic-update-slice_fusion = bf16[2,2,512,1024]{3,2,1,0:T(8,128)(2,1)} fusion(bf16[2,2,512,1024]{3,2,1,0:T(8,128)(2,1)} %constant_dynamic-update-slice_fusion.1, bf16[2,2,64,1024]{3,2,1,0:T(8,128)(2,1)} %copy-done.4), kind=kLoop, calls=%fused_computation.26 | loop fusion | bytes 1048576 | tf_op jit(solution)/shard_map/jit(_roll_dynamic)/concatenate | solution.py:105
  120.3 0.0 collective-permute-done.5
  120.3 0.0 collective-permute-done.6
  120.3 4.5 %broadcast_select_fusion.1 = (bf16[2,2,256,1024]{3,2,1,0:T(8,128)(2,1)S(1)}, bf16[2,2,256,1024]{3,2,1,0:T(8,128)(2,1)S(1)}) fusion(bf16[2,2,256,1024]{3,2,1,0:T(8,128)(2,1)} %collective-permute-done.5, pred[]{:T(512)S(6)} %eq.20, bf16[2,2,512,1024]{3,2,1,0:T(8,128)(2,1)} %constant_dynamic-update-slice_fusion, s32[]{:T(128)S(6)} %select_n.81, ...), kind=kLoop, calls=%fused_computation.10 | loop fusion | flops 2097152 | bytes 10485766 | tf_op jit(solution)/shard_map/jit(_where)/select_n | solution.py:106
  124.8 5.0 %pad_maximum_fusion.refs_0_.refs_1_.refs_2_.refs_3_.refs_4_.refs_5_.refs_6_.refs_7_ = bf16[2,6,256,1024]{3,2,1,0:T(8,128)(2,1)} fusion(bf16[2,2,256,1024]{3,2,1,0:T(8,128)(2,1)S(1)} %get-tuple-element.10, bf16[2,2,256,1024]{3,2,1,0:T(8,128)(2,1)S(1)} %copy-done.1, bf16[2,2,256,1024]{3,2,1,0:T(8,128)(2,1)S(1)} %get-tuple-element.9), kind=kLoop, calls=%fused_computation | loop fusion | flops 6291456 | bytes 12582912 | tf_op jit(solution)/shard_map/concatenate | solution.py:144
  129.9 10.5 %shard_map.73 = bf16[256,1024]{1,0:T(8,128)(2,1)} custom-call(s32[4]{0:T(128)} %clamp_bitcast_fusion.slots_ref, s32[1]{0:T(128)S(6)} %copy.15.count_ref, bf16[256,1024]{1,0:T(8,128)(2,1)} %fusion.11.q_ref, bf16[2,6,256,1024]{3,2,1,0:T(8,128)(2,1)} %pad_maximum_fusion.refs_0_.refs_1_.refs_2_.refs_3_.refs_4_.refs_5_.refs_6_.refs_7_, ...), custom_call_target="tpu_custom_call" | custom-call | tf_op jit(solution)/shard_map/pallas_call | solution.py:51
  140.4 0.0 collective-permute-done.7
  140.4 1.4 broadcast_select_fusion.3
  141.8 1.5 %fusion.14 = bf16[256,1024]{1,0:T(8,128)(2,1)} fusion(bf16[256,1024]{1,0:T(8,128)(2,1)S(1)} %copy-done.5, bf16[1024,512]{1,0:T(8,128)(2,1)S(1)} %get-tuple-element.12, bf16[1024,512]{1,0:T(8,128)(2,1)S(1)} %get-tuple-element.11), kind=kOutput, calls=%fused_computation.15 | convolution fusion | flops 541327360 | bytes 3145728 | tf_op jit(solution)/shard_map/dot_general | solution.py:147
  (15 shorter events, 0.1 us)
Async XLA Ops:
  0.0 1.9 %copy-start = (bf16[32,1024]{1,0:T(8,128)(2,1)S(1)}, bf16[32,1024]{1,0:T(8,128)(2,1)}, u32[]{:S(2)}) copy-start(bf16[32,1024]{1,0:T(8,128)(2,1)} %param.9) | copy-start | bytes 196612
  0.0 57.2 %copy-start.8 = (bf16[1024]{0:T(1024)(128)(2,1)S(1)}, bf16[1024]{0:T(1024)(128)(2,1)}, u32[]{:S(2)}) copy-start(bf16[1024]{0:T(1024)(128)(2,1)} %param.8) | copy-start | bytes 6148
  0.0 57.2 %copy-start.7 = (bf16[1024,32]{0,1:T(8,128)(2,1)S(1)}, bf16[1024,32]{0,1:T(8,128)(2,1)}, u32[]{:S(2)}) copy-start(bf16[1024,32]{0,1:T(8,128)(2,1)} %param.10) | copy-start | bytes 196612
  0.0 57.2 %copy-start.6 = (bf16[256,1024]{1,0:T(8,128)(2,1)S(1)}, bf16[256,1024]{1,0:T(8,128)(2,1)}, u32[]{:S(2)}) copy-start(bf16[256,1024]{1,0:T(8,128)(2,1)} %param.7) | copy-start | bytes 1572868
  1.2 0.8 collective-permute-start
  2.0 0.8 copy-start.2
  34.6 24.9 %collective-permute-start.1 = (bf16[1024,512]{1,0:T(8,128)(2,1)S(1)}, bf16[1024,512]{1,0:T(8,128)(2,1)S(1)}, u32[]{:S(2)}, u32[]{:S(2)}) collective-permute-start(bf16[1024,512]{1,0:T(8,128)(2,1)S(1)} %bitcast.12), channel_id=1, source_target_pairs={{0,32},{32,0},{64,96},{96,64},{128,160},{160,128},{192,224},{224,1... | collective-permute-start | bytes 3145736 | tf_op jit(solution)/shard_map/ppermute | solution.py:121
  59.7 8.3 %copy-start.1 = (bf16[2,2,256,1024]{3,2,1,0:T(8,128)(2,1)S(1)}, bf16[2,2,256,1024]{3,2,1,0:T(8,128)(2,1)}, u32[]{:S(2)}) copy-start(bf16[2,2,256,1024]{3,2,1,0:T(8,128)(2,1)} %param.11) | copy-start | bytes 6291460
  59.7 18.3 %copy-start.9 = (s32[1,4]{1,0:T(1,128)S(1)}, s32[1,4]{1,0:T(1,128)}, u32[]{:S(2)}) copy-start(s32[1,4]{1,0:T(1,128)} %param.12) | copy-start | bytes 52
  62.5 38.3 %all-to-all-start.1 = ((bf16[32,32,512]{2,1,0:T(8,128)(2,1)}), bf16[32,32,512]{2,1,0:T(8,128)(2,1)S(1)}, u32[]{:S(2)}, u32[]{:S(2)}) async-start(bf16[32,32,512]{2,1,0:T(8,128)(2,1)} %tile.5), calls=%async_computation.1 | async-start | bytes 2097152 | tf_op jit(solution)/shard_map/all_to_all | solution.py:118
  68.0 52.4 %collective-permute-start.5 = (bf16[2,2,256,1024]{3,2,1,0:T(8,128)(2,1)S(1)}, bf16[2,2,256,1024]{3,2,1,0:T(8,128)(2,1)}, u32[]{:S(2)}, u32[]{:S(2)}) collective-permute-start(bf16[2,2,256,1024]{3,2,1,0:T(8,128)(2,1)S(1)} %copy-done.1), channel_id=1, source_target_pairs={{0,32},{1,33},{2,34},{3,35},{4,36},{5,37},{6,38},{7,39},{8,40},{9,... | collective-permute-start | bytes 6291464 | tf_op jit(solution)/shard_map/ppermute | solution.py:68
  70.0 50.3 %collective-permute-start.6 = (bf16[2,2,256,1024]{3,2,1,0:T(8,128)(2,1)S(1)}, bf16[2,2,256,1024]{3,2,1,0:T(8,128)(2,1)}, u32[]{:S(2)}, u32[]{:S(2)}) collective-permute-start(bf16[2,2,256,1024]{3,2,1,0:T(8,128)(2,1)S(1)} %copy-done.1), channel_id=1, source_target_pairs={{32,0},{33,1},{34,2},{35,3},{36,4},{37,5},{38,6},{39,7},{40,8},{41... | collective-permute-start | bytes 6291464 | tf_op jit(solution)/shard_map/ppermute | solution.py:69
  73.5 6.8 %collective-permute-start.2 = (bf16[2,2,64,1024]{3,2,1,0:T(8,128)(2,1)}, bf16[2,2,64,1024]{3,2,1,0:T(8,128)(2,1)}, u32[]{:S(2)}, u32[]{:S(2)}) collective-permute-start(bf16[2,2,64,1024]{3,2,1,0:T(8,128)(2,1)} %copy-done.2), channel_id=1, source_target_pairs={{224,252},{225,253},{226,254},{227,255},{228,224},{229,225},{230,2... | collective-permute-start | bytes 1572872 | tf_op jit(solution)/shard_map/ppermute | solution.py:94
  75.0 7.2 %collective-permute-start.3 = (bf16[2,2,64,1024]{3,2,1,0:T(8,128)(2,1)}, bf16[2,2,64,1024]{3,2,1,0:T(8,128)(2,1)}, u32[]{:S(2)}, u32[]{:S(2)}) collective-permute-start(bf16[2,2,64,1024]{3,2,1,0:T(8,128)(2,1)} %copy-done.2), channel_id=1, source_target_pairs={{224,232},{225,233},{226,234},{227,235},{228,236},{229,237},{230,2... | collective-permute-start | bytes 1572872 | tf_op jit(solution)/shard_map/ppermute | solution.py:94
  77.1 7.9 %copy-start.3 = (bf16[2,2,64,1024]{3,2,1,0:T(8,128)(2,1)S(1)}, bf16[2,2,64,1024]{3,2,1,0:T(8,128)(2,1)}, u32[]{:S(2)}) copy-start(bf16[2,2,64,1024]{3,2,1,0:T(8,128)(2,1)} %copy-done.2) | copy-start | bytes 1572868
  77.1 7.0 %collective-permute-start.4 = (bf16[2,2,64,1024]{3,2,1,0:T(8,128)(2,1)}, bf16[2,2,64,1024]{3,2,1,0:T(8,128)(2,1)S(1)}, u32[]{:S(2)}, u32[]{:S(2)}) collective-permute-start(bf16[2,2,64,1024]{3,2,1,0:T(8,128)(2,1)} %copy-done.2), channel_id=1, source_target_pairs={{224,228},{225,229},{226,230},{227,231},{228,232},{229,233},{230,2... | collective-permute-start | bytes 1572872 | tf_op jit(solution)/shard_map/ppermute | solution.py:94
  84.1 1.8 %copy-start.4 = (bf16[2,2,64,1024]{3,2,1,0:T(8,128)(2,1)}, bf16[2,2,64,1024]{3,2,1,0:T(8,128)(2,1)S(1)}, u32[]{:S(2)}) copy-start(bf16[2,2,64,1024]{3,2,1,0:T(8,128)(2,1)S(1)} %collective-permute-done.4) | copy-start | bytes 1572868
  100.8 39.6 %collective-permute-start.7 = (bf16[1024,512]{1,0:T(8,128)(2,1)S(1)}, bf16[1024,512]{1,0:T(8,128)(2,1)}, u32[]{:S(2)}, u32[]{:S(2)}) collective-permute-start(bf16[1024,512]{1,0:T(8,128)(2,1)S(1)} %bitcast.11), channel_id=1, source_target_pairs={{0,32},{32,0},{64,96},{96,64},{128,160},{160,128},{192,224},{224,1... | collective-permute-start | bytes 3145736 | tf_op jit(solution)/shard_map/ppermute | solution.py:121
  140.4 1.4 %copy-start.5 = (bf16[256,1024]{1,0:T(8,128)(2,1)S(1)}, bf16[256,1024]{1,0:T(8,128)(2,1)}, u32[]{:S(2)}) copy-start(bf16[256,1024]{1,0:T(8,128)(2,1)} %shard_map.73) | copy-start | bytes 1572868
